TPU v7x, 512 devices: a whole 4x8x8 slice. The times are simulated.
512 devices in a mesh: dp: 4 (over x), ctx: 4 (over y_lo), tp: 32 (over z, y_hi, core).
Axes of the slice: x: 4, y: 8 (y_hi: 2, y_lo: 4; y = y_hi * 4 + y_lo), z: 8, core: 2. Of those that a mesh axis runs over, the one named last changes fastest.
Arguments:
- cotangent: bfloat16 [6144, 4096], P(('dp', 'ctx')), may hold values from -6 to 6
- gate_pre: bfloat16 [6144, 16384], P(('dp', 'ctx'), 'tp'), may hold values from -6 to 6
- up_pre: bfloat16 [6144, 16384], P(('dp', 'ctx'), 'tp'), may hold values from -6 to 6
- w_down: bfloat16 [4096, 16384], P(('dp', 'ctx'), 'tp'), may hold values from -0.046875 to 0.046875
Outputs:
- grad_gate: bfloat16 [6144, 16384], P(('dp', 'ctx'), 'tp')
- grad_up: bfloat16 [6144, 16384], P(('dp', 'ctx'), 'tp')
- grad_down: bfloat16 [4096, 16384], P(('dp', 'ctx'), 'tp')
All inputs are finite; a program needn't handle non-finite values.
Results may differ from a plain program's by a relative error of at most 0.018.
Values may be sent and summed in bfloat16 or wider, within the bound.
No kernel may reach another device: no remote copies, remote signals or barrier semaphores. Data moves between devices by JAX's collectives and lax.ppermute only.
A program may use at most 64 MiB of HBM per device.

v0:
```python
import jax
import jax.numpy as jnp
from jax import lax
from jax.sharding import PartitionSpec as P


def local(cotangent, gate_pre, up_pre, w_down):
    gate_wide = gate_pre.astype(jnp.float32)
    up_wide = up_pre.astype(jnp.float32)
    sigmoid_gate = jax.nn.sigmoid(gate_wide)
    activated = gate_wide * sigmoid_gate
    hidden = (activated * up_wide).astype(jnp.bfloat16)
    groups = lax.axis_size(("dp", "ctx"))
    columns = cotangent
    grad_hidden = jnp.dot(
        columns,
        lax.all_gather(w_down, ("dp", "ctx"), axis=0, tiled=True),
        preferred_element_type=jnp.float32,
    )
    grad_gate = (
        grad_hidden * up_wide * sigmoid_gate * (1.0 + gate_wide * (1.0 - sigmoid_gate))
    ).astype(jnp.bfloat16)
    grad_up = (grad_hidden * activated).astype(jnp.bfloat16)
    grad_gate, grad_up = (grad_gate, grad_up)
    columns = cotangent
    summed = lax.psum_scatter(
        lax.dot_general(
            columns, hidden, (((0,), (0,)), ((), ())), preferred_element_type=jnp.float32
        ).astype(jnp.bfloat16),
        ("dp", "ctx"),
        scatter_dimension=0,
        tiled=True,
    ).astype(jnp.float32)
    grad_down = (summed / groups).astype(jnp.bfloat16)
    return (grad_gate, grad_up, grad_down)


def solution(mesh):
    in_specs = (
        P(("dp", "ctx"), None),
        P(("dp", "ctx"), "tp"),
        P(("dp", "ctx"), "tp"),
        P(("dp", "ctx"), "tp"),
    )
    out_specs = (P(("dp", "ctx"), "tp"), P(("dp", "ctx"), "tp"), P(("dp", "ctx"), "tp"))
    return jax.shard_map(local, mesh=mesh, in_specs=in_specs, out_specs=out_specs, check_vma=False)
```

profile of v0, /device:TPU:64, one launch (start us, length us, event | category | flops | bytes accessed | tf_op | source)
XLA Modules:
  0.0 233.8 jit_solution(4152034791565453102)
XLA Ops:
  7.2 0.0 copy-start
  7.2 0.0 all-gather.2.cloned.1.call-start
  7.2 0.7 all-gather.2.cloned.1.call-update
  7.9 0.0 copy-start.1
  7.9 0.0 reduce-scatter.2.cloned.1.call-start
  8.0 1.1 copy-done
  9.1 5.5 %fusion = bf16[4096,512]{0,1:T(8,128)(2,1)} fusion(bf16[384,4096]{1,0:T(8,128)(2,1)S(1)} %copy-done, bf16[384,512]{1,0:T(8,128)(2,1)} %param.6, bf16[384,512]{1,0:T(8,128)(2,1)} %param.5), kind=kOutput, calls=%fused_computation.1 | convolution fusion | flops 1614282752 | bytes 8126464 | tf_op jit(solution)/shard_map/dot_general | solution.py:27
  14.6 0.0 reduce-scatter.2.cloned.1.call-update
  14.6 104.0 %all-gather.2.cloned.1.call-done = bf16[4096,512]{1,0:T(8,128)(2,1)} async-done(((bf16[256,512]{1,0:T(8,128)(2,1)}), bf16[4096,512]{1,0:T(8,128)(2,1)}) %all-gather.2.cloned.1.call-update) | async-done | bytes 4194320 | tf_op jit(solution)/shard_map/all_gather | solution.py:17
  118.6 0.0 copy-done.1
  118.6 5.1 %multiply_convert_fusion = (bf16[384,512]{1,0:T(8,128)(2,1)}, bf16[384,512]{1,0:T(8,128)(2,1)}) fusion(bf16[384,512]{1,0:T(8,128)(2,1)S(1)} %copy-done.1, bf16[384,512]{1,0:T(8,128)(2,1)} %param.6, bf16[384,4096]{1,0:T(8,128)(2,1)S(1)} %copy-done, bf16[4096,512]{1,0:T(8,128)(2,1)} %all-gather.2.cloned.1.call-done), kind=kOutput, calls=%fused_computation.15 | convolution fusion | flops 1613561856 | bytes 8912896 | tf_op jit(solution)/shard_map/dot_general | solution.py:15
  123.7 101.3 %reduce-scatter.2.cloned.1.call-done = bf16[256,512]{0,1:T(8,128)(2,1)} async-done(((bf16[4096,512]{0,1:T(8,128)(2,1)}), bf16[256,512]{0,1:T(8,128)(2,1)}) %reduce-scatter.2.cloned.1.call-update) | async-done | bytes 262160 | tf_op jit(solution)/shard_map/reduce_scatter | solution.py:26
  225.1 1.0 multiply_convert_fusion.1
  226.1 0.8 copy.7
Async XLA Ops:
  7.2 1.9 copy-start
  7.2 111.4 %all-gather.2.cloned.1.call-start = ((), (), s32[]{:S(2)}) async-start(), calls=%async_computation.1 | async-start | bytes 4456448 | tf_op jit(solution)/shard_map/all_gather | solution.py:17
  7.9 110.7 %copy-start.1 = (bf16[384,512]{1,0:T(8,128)(2,1)S(1)}, bf16[384,512]{1,0:T(8,128)(2,1)}, u32[]{:S(2)}) copy-start(bf16[384,512]{1,0:T(8,128)(2,1)} %param.5) | copy-start | bytes 1179652
  7.9 217.1 %reduce-scatter.2.cloned.1.call-start = ((), (), s32[]{:S(2)}) async-start(), calls=%async_computation.2 | async-start | bytes 4456448 | tf_op jit(solution)/shard_map/reduce_scatter | solution.py:26
Sparse Core Ops, SparseCore 0:
  10.1 108.4 all-gather.1
  121.4 103.5 reduce-scatter.1
where the time goes:
time: 234 us
  waiting for transfers between devices  206 us (88%)
  between operations  14.1 us (6%)
  matrix products  10.7 us (5%)
    all_gather x1, waiting for transfers between devices, local(): lax.all_gather(w_down, ('dp', 'ctx'), axis=0, tiled=True)  104 us
    reduce_scatter x1, waiting for transfers between devices, local(): lax.psum_scatter(lax.dot_general(columns, hidden, (((0,), (0,)), ((), ())...  101 us
    dot_general x1, matrix products, local(): lax.dot_general(columns, hidden, (((0,), (0,)), ((), ())), preferred_elem...  5.54 us
    dot_general x1, matrix products, local(): jnp.dot(columns, lax.all_gather(w_down, ('dp', 'ctx'), axis=0, tiled=True...  5.14 us
  transfers between devices with their start and end apart: 2, of which 2 were waited for; matrix products, arithmetic and copies ran while one was open for 5% of the time, Pallas kernels for 0%

commit v1 on v0

v1 whole, which is shorter than its diff:
```python
import jax
import jax.numpy as jnp
from jax import lax
from jax.sharding import PartitionSpec as P


def _line(x, axis, n, k):
    return lax.ppermute(x, axis, [(i, i + k) for i in range(n) if 0 <= i + k < n])


def _ring(x, axis, n, k):
    return lax.ppermute(x, axis, [(i, (i + k) % n) for i in range(n)])


def gather_line(x, axis, n):
    c = lax.axis_index(axis)
    parts = [_line(x, axis, n, n - 1 - j) if j < n - 1 else x for j in range(n)]
    parts += [_line(x, axis, n, -k) for k in range(1, n)]
    stack = jnp.stack(parts)
    out = lax.dynamic_slice_in_dim(stack, n - 1 - c, n, axis=0)
    return out.reshape((n * x.shape[0],) + x.shape[1:])


def gather_ring4(x, axis):
    h = x.shape[0] // 2
    p1 = _ring(x, axis, 4, 1)
    m1 = _ring(x, axis, 4, -1)
    f = _ring(p1[:h], axis, 4, 1)
    g = _ring(m1[h:], axis, 4, -1)
    return [x, m1, jnp.concatenate([f, g]), p1]


def scatter_ring4(blocks, axis):
    b0, b1, b2, b3 = blocks
    h = b0.shape[0] // 2
    bf = jnp.bfloat16
    s1p = _ring(b1[h:].astype(bf), axis, 4, 1)
    x1 = _ring(b2[:h].astype(bf), axis, 4, 1)
    s1m = _ring(b3[:h].astype(bf), axis, 4, -1)
    y1 = _ring(b2[h:].astype(bf), axis, 4, -1)
    s2p = _ring((b1[:h] + x1.astype(jnp.float32)).astype(bf), axis, 4, 1)
    s2m = _ring((b3[h:] + y1.astype(jnp.float32)).astype(bf), axis, 4, -1)
    f32 = jnp.float32
    top = b0[:h] + s2p.astype(f32) + s1m.astype(f32)
    bot = b0[h:] + s1p.astype(f32) + s2m.astype(f32)
    return jnp.concatenate([top, bot])


def scatter_line(x, axis, n):
    c = lax.axis_index(axis)
    rows = x.shape[0] // n
    acc = lax.dynamic_slice_in_dim(x, c * rows, rows, axis=0)
    for k in list(range(1, n)) + list(range(-n + 1, 0)):
        part = lax.dynamic_slice_in_dim(x, jnp.clip(c + k, 0, n - 1) * rows, rows, axis=0)
        acc = acc + _line(part.astype(jnp.bfloat16), axis, n, k).astype(jnp.float32)
    return acc


def local(cotangent, gate_pre, up_pre, w_down):
    gate_wide = gate_pre.astype(jnp.float32)
    up_wide = up_pre.astype(jnp.float32)
    sigmoid_gate = jax.nn.sigmoid(gate_wide)
    activated = gate_wide * sigmoid_gate
    hidden = (activated * up_wide).astype(jnp.bfloat16)
    ndp = lax.axis_size("dp")
    nctx = lax.axis_size("ctx")
    groups = ndp * nctx
    a = lax.axis_index("dp")

    w_ctx = gather_line(w_down, "ctx", nctx)
    span = w_ctx.shape[0]
    grad_hidden = None
    for k, blk in enumerate(gather_ring4(w_ctx, "dp")):
        cols = lax.dynamic_slice_in_dim(cotangent, ((a + k) % ndp) * span, span, axis=1)
        term = jnp.dot(cols, blk, preferred_element_type=jnp.float32)
        grad_hidden = term if grad_hidden is None else grad_hidden + term
    grad_gate = (
        grad_hidden * up_wide * sigmoid_gate * (1.0 + gate_wide * (1.0 - sigmoid_gate))
    ).astype(jnp.bfloat16)
    grad_up = (grad_hidden * activated).astype(jnp.bfloat16)

    partial = lax.dot_general(
        cotangent, hidden, (((0,), (0,)), ((), ())), preferred_element_type=jnp.float32
    )
    blocks = [lax.dynamic_slice_in_dim(partial, ((a + k) % ndp) * span, span, axis=0) for k in range(4)]
    reduced = scatter_ring4(blocks, "dp")
    summed = scatter_line(reduced, "ctx", nctx)
    grad_down = (summed / groups).astype(jnp.bfloat16)
    return (grad_gate, grad_up, grad_down)


def solution(mesh):
    in_specs = (
        P(("dp", "ctx"), None),
        P(("dp", "ctx"), "tp"),
        P(("dp", "ctx"), "tp"),
        P(("dp", "ctx"), "tp"),
    )
    out_specs = (P(("dp", "ctx"), "tp"), P(("dp", "ctx"), "tp"), P(("dp", "ctx"), "tp"))
    return jax.shard_map(local, mesh=mesh, in_specs=in_specs, out_specs=out_specs, check_vma=False)
```

time: 234 us -> 134 us (0.57)
  the two profiles are of different devices: /device:TPU:64 before, /device:TPU:462 now
where the time goes in v1:
time: 134 us; the launch traced here: 133 us
  starting transfers between devices  59.8 us (45%)
  waiting for transfers between devices  38.5 us (29%)
  local copies, waits for them, and re-layouts  18.2 us (14%)
  matrix products  10.8 us (8%)
  other arithmetic  4.21 us (3%)
    ppermute x10, starting transfers between devices, _ring(): return lax.ppermute(x, axis, [(i, (i + k) % n) for i in range(n)])  30.4 us
    ppermute x12, starting transfers between devices, _line(): lax.ppermute(x, axis, [(i, i + k) for i in range(n) if 0 <= i + k < n])  29.3 us
    ppermute x12, waiting for transfers between devices, _line(): lax.ppermute(x, axis, [(i, i + k) for i in range(n) if 0 <= i + k < n])  21.4 us
    ppermute x10, waiting for transfers between devices, _ring(): return lax.ppermute(x, axis, [(i, (i + k) % n) for i in range(n)])  17.2 us
    dot_general x4, matrix products, local(): term = jnp.dot(cols, blk, preferred_element_type=jnp.float32)  7.24 us
    unnamed x29, local copies, waits for them, and re-layouts  6.72 us
    dot_general x1, matrix products, local(): lax.dot_general(cotangent, hidden, (((0,), (0,)), ((), ())), preferred_el...  3.57 us
    dynamic_slice x1, local copies, waits for them, and re-layouts, local(): lax.dynamic_slice_in_dim(partial, (a + k) % ndp * span, span, axis=0)  2.76 us
  transfers between devices with their start and end apart: 22, of which 10 were waited for; matrix products, arithmetic and copies ran while one was open for 23% of the time, Pallas kernels for 0%

profile of v1, /device:TPU:462, one launch (start us, length us, event | category | flops | bytes accessed | tf_op | source)
XLA Modules:
  0.0 132.6 jit_solution(8911673303175270229)
XLA Ops:
  0.6 1.5 %collective-permute-start = (bf16[256,512]{1,0:T(8,128)(2,1)}, bf16[256,512]{1,0:T(8,128)(2,1)}, u32[]{:S(2)}, u32[]{:S(2)}) collective-permute-start(bf16[256,512]{1,0:T(8,128)(2,1)} %param.7), channel_id=1, source_target_pairs={{0,96},{1,97},{2,98},{3,99},{4,100},{5,101},{6,102},{7,103},{8,104... | collective-permute-start | bytes 786440 | tf_op jit(solution)/shard_map/ppermute | solution.py:8
  2.2 5.2 %collective-permute-start.1 = (bf16[256,512]{1,0:T(8,128)(2,1)}, bf16[256,512]{1,0:T(8,128)(2,1)}, u32[]{:S(2)}, u32[]{:S(2)}) collective-permute-start(bf16[256,512]{1,0:T(8,128)(2,1)} %param.7), channel_id=1, source_target_pairs={{0,64},{32,96},{1,65},{33,97},{2,66},{34,98},{3,67},{35,99},{4,68}... | collective-permute-start | bytes 786440 | tf_op jit(solution)/shard_map/ppermute | solution.py:8
  7.4 1.9 %collective-permute-start.2 = (bf16[256,512]{1,0:T(8,128)(2,1)}, bf16[256,512]{1,0:T(8,128)(2,1)}, u32[]{:S(2)}, u32[]{:S(2)}) collective-permute-start(bf16[256,512]{1,0:T(8,128)(2,1)} %param.7), channel_id=1, source_target_pairs={{0,32},{32,64},{64,96},{1,33},{33,65},{65,97},{2,34},{34,66},{66,9... | collective-permute-start | bytes 786440 | tf_op jit(solution)/shard_map/ppermute | solution.py:8
  9.3 4.6 %collective-permute-start.3 = (bf16[256,512]{1,0:T(8,128)(2,1)}, bf16[256,512]{1,0:T(8,128)(2,1)}, u32[]{:S(2)}, u32[]{:S(2)}) collective-permute-start(bf16[256,512]{1,0:T(8,128)(2,1)} %param.7), channel_id=1, source_target_pairs={{32,0},{64,32},{96,64},{33,1},{65,33},{97,65},{34,2},{66,34},{98,6... | collective-permute-start | bytes 786440 | tf_op jit(solution)/shard_map/ppermute | solution.py:8
  13.9 1.3 collective-permute-start.4
  15.3 3.6 %fusion.44 = f32[512,4096]{1,0:T(8,128)S(1)} fusion(bf16[384,4096]{1,0:T(8,128)(2,1)S(1)} %copy-done, bf16[384,512]{1,0:T(8,128)(2,1)} %param.6, bf16[384,512]{1,0:T(8,128)(2,1)} %param.5), kind=kOutput, calls=%fused_computation.76 | convolution fusion | flops 1612185600 | bytes 12320768 | tf_op jit(solution)/shard_map/dot_general | solution.py:82
  19.1 2.8 %dynamic-slice_bitcast_fusion.1 = (f32[1024,512]{0,1:T(8,128)}, f32[1024,512]{0,1:T(8,128)}, f32[1024,512]{0,1:T(8,128)}) fusion(f32[512,4096]{1,0:T(8,128)S(1)} %fusion.44, s32[]{:T(128)S(6)} %select_n.71, s32[]{:T(128)S(6)} %select_n.75, s32[]{:T(128)S(6)} %select_n.68), kind=kLoop, calls=%fused_computation.16 | loop fusion | bytes 12582924 | tf_op jit(solution)/shard_map/dynamic_slice | solution.py:85
  21.8 1.1 fusion.52
  22.9 2.1 %slice.69 = bf16[512,512]{0,1:T(8,128)(2,1)} slice(f32[1024,512]{0,1:T(8,128)} %get-tuple-element.7), slice={[0:512], [0:512]} | slice | bytes 1048576 | tf_op jit(solution)/shard_map/slice | solution.py:39
  25.0 2.1 %slice.68 = bf16[512,512]{0,1:T(8,128)(2,1)} slice(f32[1024,512]{0,1:T(8,128)} %get-tuple-element.6), slice={[512:1024], [0:512]} | slice | bytes 1048576 | tf_op jit(solution)/shard_map/slice | solution.py:37
  27.9 1.0 bitcast_dynamic-update-slice_fusion.6
  28.9 2.5 %collective-permute-start.10 = (bf16[512,512]{0,1:T(8,128)(2,1)}, bf16[512,512]{0,1:T(8,128)(2,1)S(1)}, u32[]{:S(2)}, u32[]{:S(2)}) collective-permute-start(bf16[512,512]{0,1:T(8,128)(2,1)} %get-tuple-element.20), channel_id=1, source_target_pairs={{0,128},{128,256},{256,384},{384,0},{1,129},{129,257},{257,385},{3... | collective-permute-start | bytes 1572872 | tf_op jit(solution)/shard_map/ppermute | solution.py:12
  31.5 1.0 bitcast_dynamic-update-slice_fusion.5
  32.4 3.5 %collective-permute-start.14 = (bf16[512,512]{0,1:T(8,128)(2,1)}, bf16[512,512]{0,1:T(8,128)(2,1)S(1)}, u32[]{:S(2)}, u32[]{:S(2)}) collective-permute-start(bf16[512,512]{0,1:T(8,128)(2,1)} %get-tuple-element.19), channel_id=1, source_target_pairs={{0,384},{128,0},{256,128},{384,256},{1,385},{129,1},{257,129},{385... | collective-permute-start | bytes 1572872 | tf_op jit(solution)/shard_map/ppermute | solution.py:12
  35.9 1.0 bitcast_dynamic-update-slice_fusion.4
  36.9 2.7 %collective-permute-start.12 = (bf16[512,512]{0,1:T(8,128)(2,1)}, bf16[512,512]{0,1:T(8,128)(2,1)S(1)}, u32[]{:S(2)}, u32[]{:S(2)}) collective-permute-start(bf16[512,512]{0,1:T(8,128)(2,1)} %slice.69), channel_id=1, source_target_pairs={{0,384},{128,0},{256,128},{384,256},{1,385},{129,1},{257,129},{385... | collective-permute-start | bytes 1572872 | tf_op jit(solution)/shard_map/ppermute | solution.py:12
  39.7 1.0 bitcast_dynamic-update-slice_fusion.2
  40.6 3.4 %collective-permute-done.10 = bf16[512,512]{0,1:T(8,128)(2,1)S(1)} collective-permute-done((bf16[512,512]{0,1:T(8,128)(2,1)}, bf16[512,512]{0,1:T(8,128)(2,1)S(1)}, u32[]{:S(2)}, u32[]{:S(2)}) %collective-permute-start.10) | collective-permute-done | bytes 524320 | tf_op jit(solution)/shard_map/ppermute | solution.py:12
  44.0 3.6 %collective-permute-start.13 = (bf16[512,512]{0,1:T(8,128)(2,1)S(1)}, bf16[512,512]{0,1:T(8,128)(2,1)S(1)}, u32[]{:S(2)}, u32[]{:S(2)}) collective-permute-start(bf16[512,512]{0,1:T(8,128)(2,1)S(1)} %copy-done.6), channel_id=1, source_target_pairs={{0,128},{128,256},{256,384},{384,0},{1,129},{129,257},{257,385},{3... | collective-permute-start | bytes 1572872 | tf_op jit(solution)/shard_map/ppermute | solution.py:12
  47.8 2.8 %collective-permute-done.14 = bf16[512,512]{0,1:T(8,128)(2,1)S(1)} collective-permute-done((bf16[512,512]{0,1:T(8,128)(2,1)}, bf16[512,512]{0,1:T(8,128)(2,1)S(1)}, u32[]{:S(2)}, u32[]{:S(2)}) %collective-permute-start.14) | collective-permute-done | bytes 524320 | tf_op jit(solution)/shard_map/ppermute | solution.py:12
  50.6 2.2 %collective-permute-start.11 = (bf16[512,512]{0,1:T(8,128)(2,1)S(1)}, bf16[512,512]{0,1:T(8,128)(2,1)S(1)}, u32[]{:S(2)}, u32[]{:S(2)}) collective-permute-start(bf16[512,512]{0,1:T(8,128)(2,1)S(1)} %fusion.4), channel_id=1, source_target_pairs={{0,128},{128,256},{256,384},{384,0},{1,129},{129,257},{257,385},{3... | collective-permute-start | bytes 1572872 | tf_op jit(solution)/shard_map/ppermute | solution.py:12
  53.0 3.8 %collective-permute-start.15 = (bf16[512,512]{0,1:T(8,128)(2,1)S(1)}, bf16[512,512]{0,1:T(8,128)(2,1)S(1)}, u32[]{:S(2)}, u32[]{:S(2)}) collective-permute-start(bf16[512,512]{0,1:T(8,128)(2,1)S(1)} %fusion.2), channel_id=1, source_target_pairs={{0,384},{128,0},{256,128},{384,256},{1,385},{129,1},{257,129},{385... | collective-permute-start | bytes 1572872 | tf_op jit(solution)/shard_map/ppermute | solution.py:12
  56.8 1.0 bitcast_dynamic-update-slice_fusion.1
  57.8 1.1 constant_dynamic-slice_fusion
  58.9 2.2 %collective-permute-start.6 = (bf16[1024,512]{1,0:T(8,128)(2,1)}, bf16[1024,512]{1,0:T(8,128)(2,1)}, u32[]{:S(2)}, u32[]{:S(2)}) collective-permute-start(bf16[1024,512]{1,0:T(8,128)(2,1)} %bitcast.7), channel_id=1, source_target_pairs={{0,384},{128,0},{256,128},{384,256},{1,385},{129,1},{257,129},{385... | collective-permute-start | bytes 3145736 | tf_op jit(solution)/shard_map/ppermute | solution.py:12
  61.9 4.1 %collective-permute-start.7 = (bf16[1024,512]{1,0:T(8,128)(2,1)}, bf16[1024,512]{1,0:T(8,128)(2,1)}, u32[]{:S(2)}, u32[]{:S(2)}) collective-permute-start(bf16[1024,512]{1,0:T(8,128)(2,1)} %bitcast.7), channel_id=1, source_target_pairs={{0,128},{128,256},{256,384},{384,0},{1,129},{129,257},{257,385},{3... | collective-permute-start | bytes 3145736 | tf_op jit(solution)/shard_map/ppermute | solution.py:12
  66.0 6.0 %collective-permute-done.11 = bf16[512,512]{0,1:T(8,128)(2,1)S(1)} collective-permute-done((bf16[512,512]{0,1:T(8,128)(2,1)S(1)}, bf16[512,512]{0,1:T(8,128)(2,1)S(1)}, u32[]{:S(2)}, u32[]{:S(2)}) %collective-permute-start.11) | collective-permute-done | bytes 524320 | tf_op jit(solution)/shard_map/ppermute | solution.py:12
  72.0 1.1 collective-permute-done.15
  74.5 1.7 %fusion.34 = (bf16[256,512]{0,1:T(8,128)(2,1)S(1)}, bf16[256,512]{0,1:T(8,128)(2,1)S(1)}, bf16[256,512]{0,1:T(8,128)(2,1)S(1)}, bf16[256,512]{0,1:T(8,128)(2,1)}...) fusion(s32[]{:T(128)S(6)} %select_n.77, f32[512,512]{0,1:T(8,128)S(1)} %get-tuple-element.16, ...), kind=kLoop, calls=%fused_computation.66 | loop fusion | flops 3145728 | bytes 3670040 | tf_op jit(solution)/shard_map/convert_element_type | solution.py:55
  76.2 4.0 %collective-permute-start.16 = (bf16[256,512]{0,1:T(8,128)(2,1)S(1)}, bf16[256,512]{0,1:T(8,128)(2,1)}, u32[]{:S(2)}, u32[]{:S(2)}) collective-permute-start(bf16[256,512]{0,1:T(8,128)(2,1)S(1)} %get-tuple-element.9), channel_id=1, source_target_pairs={{0,32},{32,64},{64,96},{1,33},{33,65},{65,97},{2,34},{34,66},{66,9... | collective-permute-start | bytes 786440 | tf_op jit(solution)/shard_map/ppermute | solution.py:8
  80.2 4.7 %collective-permute-start.17 = (bf16[256,512]{0,1:T(8,128)(2,1)S(1)}, bf16[256,512]{0,1:T(8,128)(2,1)}, u32[]{:S(2)}, u32[]{:S(2)}) collective-permute-start(bf16[256,512]{0,1:T(8,128)(2,1)S(1)} %get-tuple-element.10), channel_id=1, source_target_pairs={{0,64},{32,96},{1,65},{33,97},{2,66},{34,98},{3,67},{35,99},{4,68}... | collective-permute-start | bytes 786440 | tf_op jit(solution)/shard_map/ppermute | solution.py:8
  84.9 1.3 %collective-permute-start.18 = (bf16[256,512]{0,1:T(8,128)(2,1)S(1)}, bf16[256,512]{0,1:T(8,128)(2,1)}, u32[]{:S(2)}, u32[]{:S(2)}) collective-permute-start(bf16[256,512]{0,1:T(8,128)(2,1)S(1)} %get-tuple-element.11), channel_id=1, source_target_pairs={{0,96},{1,97},{2,98},{3,99},{4,100},{5,101},{6,102},{7,103},{8,104... | collective-permute-start | bytes 786440 | tf_op jit(solution)/shard_map/ppermute | solution.py:8
  86.3 9.8 %collective-permute-done.16 = bf16[256,512]{0,1:T(8,128)(2,1)} collective-permute-done((bf16[256,512]{0,1:T(8,128)(2,1)S(1)}, bf16[256,512]{0,1:T(8,128)(2,1)}, u32[]{:S(2)}, u32[]{:S(2)}) %collective-permute-start.16) | collective-permute-done | bytes 262176 | tf_op jit(solution)/shard_map/ppermute | solution.py:8
  96.8 2.1 %collective-permute-done.17 = bf16[256,512]{0,1:T(8,128)(2,1)} collective-permute-done((bf16[256,512]{0,1:T(8,128)(2,1)S(1)}, bf16[256,512]{0,1:T(8,128)(2,1)}, u32[]{:S(2)}, u32[]{:S(2)}) %collective-permute-start.17) | collective-permute-done | bytes 262176 | tf_op jit(solution)/shard_map/ppermute | solution.py:8
  98.9 1.3 collective-permute-start.20
  100.2 1.9 %collective-permute-start.21 = (bf16[256,512]{0,1:T(8,128)(2,1)}, bf16[256,512]{0,1:T(8,128)(2,1)}, u32[]{:S(2)}, u32[]{:S(2)}) collective-permute-start(bf16[256,512]{0,1:T(8,128)(2,1)} %get-tuple-element.14), channel_id=1, source_target_pairs={{32,0},{64,32},{96,64},{33,1},{65,33},{97,65},{34,2},{66,34},{98,6... | collective-permute-start | bytes 786440 | tf_op jit(solution)/shard_map/ppermute | solution.py:8
  102.2 6.3 %collective-permute-done.20 = bf16[256,512]{0,1:T(8,128)(2,1)} collective-permute-done((bf16[256,512]{0,1:T(8,128)(2,1)}, bf16[256,512]{0,1:T(8,128)(2,1)}, u32[]{:S(2)}, u32[]{:S(2)}) %collective-permute-start.20) | collective-permute-done | bytes 262176 | tf_op jit(solution)/shard_map/ppermute | solution.py:8
  108.5 3.0 %collective-permute-done.21 = bf16[256,512]{0,1:T(8,128)(2,1)} collective-permute-done((bf16[256,512]{0,1:T(8,128)(2,1)}, bf16[256,512]{0,1:T(8,128)(2,1)}, u32[]{:S(2)}, u32[]{:S(2)}) %collective-permute-start.21) | collective-permute-done | bytes 262176 | tf_op jit(solution)/shard_map/ppermute | solution.py:8
  111.5 1.8 %fusion.43 = bf16[256,512]{0,1:T(8,128)(2,1)S(1)} fusion(bf16[256,512]{0,1:T(8,128)(2,1)} %collective-permute-done.21, bf16[256,512]{0,1:T(8,128)(2,1)} %collective-permute-done.20, bf16[256,512]{0,1:T(8,128)(2,1)} %copy-done.9, bf16[256,512]{0,1:T(8,128)(2,1)} %collective-permute-done.18, bf16[256,512]{0,1:T(8,128)(2,1)} %collective-permute-done.17, ...), kind=kLoop, calls=%fused_computation.75 | loop fusion | flops 1966080 | bytes 3932164 | tf_op jit(solution)/shard_map/convert_element_type | solution.py:88
  114.2 1.1 slice.44
  115.3 2.2 %collective-permute-start.8 = (bf16[512,512]{1,0:T(8,128)(2,1)S(1)}, bf16[512,512]{1,0:T(8,128)(2,1)S(1)}, u32[]{:S(2)}, u32[]{:S(2)}) collective-permute-start(bf16[512,512]{1,0:T(8,128)(2,1)S(1)} %slice.44), channel_id=1, source_target_pairs={{0,128},{128,256},{256,384},{384,0},{1,129},{129,257},{257,385},{3... | collective-permute-start | bytes 1572872 | tf_op jit(solution)/shard_map/ppermute | solution.py:12
  117.5 1.1 slice.45
  118.5 3.6 %collective-permute-start.9 = (bf16[512,512]{1,0:T(8,128)(2,1)S(1)}, bf16[512,512]{1,0:T(8,128)(2,1)S(1)}, u32[]{:S(2)}, u32[]{:S(2)}) collective-permute-start(bf16[512,512]{1,0:T(8,128)(2,1)S(1)} %slice.45), channel_id=1, source_target_pairs={{0,384},{128,0},{256,128},{384,256},{1,385},{129,1},{257,129},{385... | collective-permute-start | bytes 1572872 | tf_op jit(solution)/shard_map/ppermute | solution.py:12
  122.2 1.8 %fusion.20 = f32[384,512]{1,0:T(8,128)S(1)} fusion(bf16[1024,512]{1,0:T(8,128)(2,1)} %collective-permute-done.6, bf16[384,4096]{1,0:T(8,128)(2,1)S(1)} %copy-done, s32[]{:T(128)S(6)} %select_n.71), kind=kOutput, calls=%fused_computation.52 | convolution fusion | flops 402653184 | bytes 2621444 | tf_op jit(solution)/shard_map/dot_general | solution.py:75
  124.0 1.8 %fusion.17 = f32[384,512]{1,0:T(8,128)S(1)} fusion(bf16[1024,512]{1,0:T(8,128)(2,1)} %collective-permute-done.7, bf16[384,4096]{1,0:T(8,128)(2,1)S(1)} %copy-done, s32[]{:T(128)S(6)} %select_n.75), kind=kOutput, calls=%fused_computation.49 | convolution fusion | flops 402653184 | bytes 2621444 | tf_op jit(solution)/shard_map/dot_general | solution.py:75
  125.8 1.9 %convolution_add_fusion.1 = f32[384,512]{1,0:T(8,128)S(1)} fusion(f32[384,512]{1,0:T(8,128)S(1)} %fusion.20, bf16[1024,512]{1,0:T(8,128)(2,1)} %bitcast.7, bf16[384,4096]{1,0:T(8,128)(2,1)S(1)} %copy-done, s32[]{:T(128)S(6)} %select_n.68), kind=kOutput, calls=%fused_computation.19 | convolution fusion | flops 402849792 | bytes 3407876 | tf_op jit(solution)/shard_map/dot_general | solution.py:75
  127.7 3.1 %collective-permute-done.9 = bf16[512,512]{1,0:T(8,128)(2,1)S(1)} collective-permute-done((bf16[512,512]{1,0:T(8,128)(2,1)S(1)}, bf16[512,512]{1,0:T(8,128)(2,1)S(1)}, u32[]{:S(2)}, u32[]{:S(2)}) %collective-permute-start.9) | collective-permute-done | bytes 524320 | tf_op jit(solution)/shard_map/ppermute | solution.py:12
  130.8 1.8 %multiply_convert_fusion = (bf16[384,512]{1,0:T(8,128)(2,1)}, bf16[384,512]{1,0:T(8,128)(2,1)}) fusion(bf16[384,512]{1,0:T(8,128)(2,1)S(1)} %copy-done.7, bf16[384,512]{1,0:T(8,128)(2,1)S(1)} %copy-done.8, f32[384,512]{1,0:T(8,128)S(1)} %fusion.17, f32[384,512]{1,0:T(8,128)S(1)} %convolution_add_fusion.1, bf16[512,512]{1,0:T(8,128)(2,1)S(1)} %collective-permute-done.9, ...), kind=kOutput, calls=%fused_computation.48 | convolution fusion | flops 408092672 | bytes 4980740 | tf_op jit(solution)/shard_map/dot_general | solution.py:75
  (44 shorter events, 5.0 us)
Async XLA Ops:
  0.6 14.7 %copy-start = (bf16[384,4096]{1,0:T(8,128)(2,1)S(1)}, bf16[384,4096]{1,0:T(8,128)(2,1)}, u32[]{:S(2)}) copy-start(bf16[384,4096]{1,0:T(8,128)(2,1)} %param.4) | copy-start | bytes 9437188
  0.6 26.5 %collective-permute-start = (bf16[256,512]{1,0:T(8,128)(2,1)}, bf16[256,512]{1,0:T(8,128)(2,1)}, u32[]{:S(2)}, u32[]{:S(2)}) collective-permute-start(bf16[256,512]{1,0:T(8,128)(2,1)} %param.7), channel_id=1, source_target_pairs={{0,96},{1,97},{2,98},{3,99},{4,100},{5,101},{6,102},{7,103},{8,104... | collective-permute-start | bytes 786440 | tf_op jit(solution)/shard_map/ppermute | solution.py:8
  2.2 26.7 %collective-permute-start.1 = (bf16[256,512]{1,0:T(8,128)(2,1)}, bf16[256,512]{1,0:T(8,128)(2,1)}, u32[]{:S(2)}, u32[]{:S(2)}) collective-permute-start(bf16[256,512]{1,0:T(8,128)(2,1)} %param.7), channel_id=1, source_target_pairs={{0,64},{32,96},{1,65},{33,97},{2,66},{34,98},{3,67},{35,99},{4,68}... | collective-permute-start | bytes 786440 | tf_op jit(solution)/shard_map/ppermute | solution.py:8
  7.4 25.0 %collective-permute-start.2 = (bf16[256,512]{1,0:T(8,128)(2,1)}, bf16[256,512]{1,0:T(8,128)(2,1)}, u32[]{:S(2)}, u32[]{:S(2)}) collective-permute-start(bf16[256,512]{1,0:T(8,128)(2,1)} %param.7), channel_id=1, source_target_pairs={{0,32},{32,64},{64,96},{1,33},{33,65},{65,97},{2,34},{34,66},{66,9... | collective-permute-start | bytes 786440 | tf_op jit(solution)/shard_map/ppermute | solution.py:8
  9.3 27.6 %collective-permute-start.3 = (bf16[256,512]{1,0:T(8,128)(2,1)}, bf16[256,512]{1,0:T(8,128)(2,1)}, u32[]{:S(2)}, u32[]{:S(2)}) collective-permute-start(bf16[256,512]{1,0:T(8,128)(2,1)} %param.7), channel_id=1, source_target_pairs={{32,0},{64,32},{96,64},{33,1},{65,33},{97,65},{34,2},{66,34},{98,6... | collective-permute-start | bytes 786440 | tf_op jit(solution)/shard_map/ppermute | solution.py:8
  13.9 39.1 %collective-permute-start.4 = (bf16[256,512]{1,0:T(8,128)(2,1)}, bf16[256,512]{1,0:T(8,128)(2,1)}, u32[]{:S(2)}, u32[]{:S(2)}) collective-permute-start(bf16[256,512]{1,0:T(8,128)(2,1)} %param.7), channel_id=1, source_target_pairs={{64,0},{96,32},{65,1},{97,33},{66,2},{98,34},{67,3},{99,35},{68,4}... | collective-permute-start | bytes 786440 | tf_op jit(solution)/shard_map/ppermute | solution.py:8
  21.8 5.3 %copy-start.10 = (bf16[256,512]{1,0:T(8,128)(2,1)S(1)}, bf16[256,512]{1,0:T(8,128)(2,1)}, u32[]{:S(2)}) copy-start(bf16[256,512]{1,0:T(8,128)(2,1)} %param.7) | copy-start | bytes 786436
  27.1 16.9 %copy-start.6 = (bf16[512,512]{0,1:T(8,128)(2,1)S(1)}, bf16[512,512]{0,1:T(8,128)(2,1)}, u32[]{:S(2)}) copy-start(bf16[512,512]{0,1:T(8,128)(2,1)} %slice.68) | copy-start | bytes 1572868
  27.1 20.5 %copy-start.5 = (f32[1024,512]{0,1:T(8,128)S(1)}, f32[1024,512]{0,1:T(8,128)}, u32[]{:S(2)}) copy-start(f32[1024,512]{0,1:T(8,128)} %get-tuple-element.6) | copy-start | bytes 6291460
  27.1 30.6 %collective-permute-start.5 = (bf16[256,512]{1,0:T(8,128)(2,1)S(1)}, bf16[256,512]{1,0:T(8,128)(2,1)S(1)}, u32[]{:S(2)}, u32[]{:S(2)}) collective-permute-start(bf16[256,512]{1,0:T(8,128)(2,1)S(1)} %copy-done.10), channel_id=1, source_target_pairs={{96,0},{97,1},{98,2},{99,3},{100,4},{101,5},{102,6},{103,7},{104,8... | collective-permute-start | bytes 786440 | tf_op jit(solution)/shard_map/ppermute | solution.py:8
  28.9 23.9 %copy-start.4 = (f32[1024,512]{0,1:T(8,128)S(1)}, f32[1024,512]{0,1:T(8,128)}, u32[]{:S(2)}) copy-start(f32[1024,512]{0,1:T(8,128)} %get-tuple-element.7) | copy-start | bytes 6291460
  28.9 15.1 %collective-permute-start.10 = (bf16[512,512]{0,1:T(8,128)(2,1)}, bf16[512,512]{0,1:T(8,128)(2,1)S(1)}, u32[]{:S(2)}, u32[]{:S(2)}) collective-permute-start(bf16[512,512]{0,1:T(8,128)(2,1)} %get-tuple-element.20), channel_id=1, source_target_pairs={{0,128},{128,256},{256,384},{384,0},{1,129},{129,257},{257,385},{3... | collective-permute-start | bytes 1572872 | tf_op jit(solution)/shard_map/ppermute | solution.py:12
  32.4 18.2 %collective-permute-start.14 = (bf16[512,512]{0,1:T(8,128)(2,1)}, bf16[512,512]{0,1:T(8,128)(2,1)S(1)}, u32[]{:S(2)}, u32[]{:S(2)}) collective-permute-start(bf16[512,512]{0,1:T(8,128)(2,1)} %get-tuple-element.19), channel_id=1, source_target_pairs={{0,384},{128,0},{256,128},{384,256},{1,385},{129,1},{257,129},{385... | collective-permute-start | bytes 1572872 | tf_op jit(solution)/shard_map/ppermute | solution.py:12
  36.9 24.9 %collective-permute-start.12 = (bf16[512,512]{0,1:T(8,128)(2,1)}, bf16[512,512]{0,1:T(8,128)(2,1)S(1)}, u32[]{:S(2)}, u32[]{:S(2)}) collective-permute-start(bf16[512,512]{0,1:T(8,128)(2,1)} %slice.69), channel_id=1, source_target_pairs={{0,384},{128,0},{256,128},{384,256},{1,385},{129,1},{257,129},{385... | collective-permute-start | bytes 1572872 | tf_op jit(solution)/shard_map/ppermute | solution.py:12
  44.0 22.0 %collective-permute-start.13 = (bf16[512,512]{0,1:T(8,128)(2,1)S(1)}, bf16[512,512]{0,1:T(8,128)(2,1)S(1)}, u32[]{:S(2)}, u32[]{:S(2)}) collective-permute-start(bf16[512,512]{0,1:T(8,128)(2,1)S(1)} %copy-done.6), channel_id=1, source_target_pairs={{0,128},{128,256},{256,384},{384,0},{1,129},{129,257},{257,385},{3... | collective-permute-start | bytes 1572872 | tf_op jit(solution)/shard_map/ppermute | solution.py:12
  50.6 21.4 %collective-permute-start.11 = (bf16[512,512]{0,1:T(8,128)(2,1)S(1)}, bf16[512,512]{0,1:T(8,128)(2,1)S(1)}, u32[]{:S(2)}, u32[]{:S(2)}) collective-permute-start(bf16[512,512]{0,1:T(8,128)(2,1)S(1)} %fusion.4), channel_id=1, source_target_pairs={{0,128},{128,256},{256,384},{384,0},{1,129},{129,257},{257,385},{3... | collective-permute-start | bytes 1572872 | tf_op jit(solution)/shard_map/ppermute | solution.py:12
  53.0 20.1 %copy-start.3 = (f32[1024,512]{0,1:T(8,128)S(1)}, f32[1024,512]{0,1:T(8,128)}, u32[]{:S(2)}) copy-start(f32[1024,512]{0,1:T(8,128)} %get-tuple-element.8) | copy-start | bytes 6291460
  53.0 20.1 %collective-permute-start.15 = (bf16[512,512]{0,1:T(8,128)(2,1)S(1)}, bf16[512,512]{0,1:T(8,128)(2,1)S(1)}, u32[]{:S(2)}, u32[]{:S(2)}) collective-permute-start(bf16[512,512]{0,1:T(8,128)(2,1)S(1)} %fusion.2), channel_id=1, source_target_pairs={{0,384},{128,0},{256,128},{384,256},{1,385},{129,1},{257,129},{385... | collective-permute-start | bytes 1572872 | tf_op jit(solution)/shard_map/ppermute | solution.py:12
  58.9 58.6 %collective-permute-start.6 = (bf16[1024,512]{1,0:T(8,128)(2,1)}, bf16[1024,512]{1,0:T(8,128)(2,1)}, u32[]{:S(2)}, u32[]{:S(2)}) collective-permute-start(bf16[1024,512]{1,0:T(8,128)(2,1)} %bitcast.7), channel_id=1, source_target_pairs={{0,384},{128,0},{256,128},{384,256},{1,385},{129,1},{257,129},{385... | collective-permute-start | bytes 3145736 | tf_op jit(solution)/shard_map/ppermute | solution.py:12
  61.9 52.3 %collective-permute-start.7 = (bf16[1024,512]{1,0:T(8,128)(2,1)}, bf16[1024,512]{1,0:T(8,128)(2,1)}, u32[]{:S(2)}, u32[]{:S(2)}) collective-permute-start(bf16[1024,512]{1,0:T(8,128)(2,1)} %bitcast.7), channel_id=1, source_target_pairs={{0,128},{128,256},{256,384},{384,0},{1,129},{129,257},{257,385},{3... | collective-permute-start | bytes 3145736 | tf_op jit(solution)/shard_map/ppermute | solution.py:12
  73.5 1.0 copy-start.1
  73.5 2.6 %copy-start.2 = (f32[512,512]{0,1:T(8,128)}, f32[512,512]{0,1:T(8,128)S(1)}, u32[]{:S(2)}) copy-start(f32[512,512]{0,1:T(8,128)S(1)} %get-tuple-element.16) | copy-start | bytes 3145732
  76.2 19.9 %collective-permute-start.16 = (bf16[256,512]{0,1:T(8,128)(2,1)S(1)}, bf16[256,512]{0,1:T(8,128)(2,1)}, u32[]{:S(2)}, u32[]{:S(2)}) collective-permute-start(bf16[256,512]{0,1:T(8,128)(2,1)S(1)} %get-tuple-element.9), channel_id=1, source_target_pairs={{0,32},{32,64},{64,96},{1,33},{33,65},{65,97},{2,34},{34,66},{66,9... | collective-permute-start | bytes 786440 | tf_op jit(solution)/shard_map/ppermute | solution.py:8
  80.2 18.7 %collective-permute-start.17 = (bf16[256,512]{0,1:T(8,128)(2,1)S(1)}, bf16[256,512]{0,1:T(8,128)(2,1)}, u32[]{:S(2)}, u32[]{:S(2)}) collective-permute-start(bf16[256,512]{0,1:T(8,128)(2,1)S(1)} %get-tuple-element.10), channel_id=1, source_target_pairs={{0,64},{32,96},{1,65},{33,97},{2,66},{34,98},{3,67},{35,99},{4,68}... | collective-permute-start | bytes 786440 | tf_op jit(solution)/shard_map/ppermute | solution.py:8
  84.9 15.3 %collective-permute-start.18 = (bf16[256,512]{0,1:T(8,128)(2,1)S(1)}, bf16[256,512]{0,1:T(8,128)(2,1)}, u32[]{:S(2)}, u32[]{:S(2)}) collective-permute-start(bf16[256,512]{0,1:T(8,128)(2,1)S(1)} %get-tuple-element.11), channel_id=1, source_target_pairs={{0,96},{1,97},{2,98},{3,99},{4,100},{5,101},{6,102},{7,103},{8,104... | collective-permute-start | bytes 786440 | tf_op jit(solution)/shard_map/ppermute | solution.py:8
  96.1 6.0 %collective-permute-start.19 = (bf16[256,512]{0,1:T(8,128)(2,1)}, bf16[256,512]{0,1:T(8,128)(2,1)S(1)}, u32[]{:S(2)}, u32[]{:S(2)}) collective-permute-start(bf16[256,512]{0,1:T(8,128)(2,1)} %get-tuple-element.12), channel_id=1, source_target_pairs={{96,0},{97,1},{98,2},{99,3},{100,4},{101,5},{102,6},{103,7},{104,8... | collective-permute-start | bytes 786440 | tf_op jit(solution)/shard_map/ppermute | solution.py:8
  98.9 9.6 %collective-permute-start.20 = (bf16[256,512]{0,1:T(8,128)(2,1)}, bf16[256,512]{0,1:T(8,128)(2,1)}, u32[]{:S(2)}, u32[]{:S(2)}) collective-permute-start(bf16[256,512]{0,1:T(8,128)(2,1)} %get-tuple-element.13), channel_id=1, source_target_pairs={{64,0},{96,32},{65,1},{97,33},{66,2},{98,34},{67,3},{99,35},{68,4}... | collective-permute-start | bytes 786440 | tf_op jit(solution)/shard_map/ppermute | solution.py:8
  100.2 11.3 %collective-permute-start.21 = (bf16[256,512]{0,1:T(8,128)(2,1)}, bf16[256,512]{0,1:T(8,128)(2,1)}, u32[]{:S(2)}, u32[]{:S(2)}) collective-permute-start(bf16[256,512]{0,1:T(8,128)(2,1)} %get-tuple-element.14), channel_id=1, source_target_pairs={{32,0},{64,32},{96,64},{33,1},{65,33},{97,65},{34,2},{66,34},{98,6... | collective-permute-start | bytes 786440 | tf_op jit(solution)/shard_map/ppermute | solution.py:8
  102.1 6.3 %copy-start.9 = (bf16[256,512]{0,1:T(8,128)(2,1)}, bf16[256,512]{0,1:T(8,128)(2,1)S(1)}, u32[]{:S(2)}) copy-start(bf16[256,512]{0,1:T(8,128)(2,1)S(1)} %collective-permute-done.19) | copy-start | bytes 786436
  115.3 12.5 %collective-permute-start.8 = (bf16[512,512]{1,0:T(8,128)(2,1)S(1)}, bf16[512,512]{1,0:T(8,128)(2,1)S(1)}, u32[]{:S(2)}, u32[]{:S(2)}) collective-permute-start(bf16[512,512]{1,0:T(8,128)(2,1)S(1)} %slice.44), channel_id=1, source_target_pairs={{0,128},{128,256},{256,384},{384,0},{1,129},{129,257},{257,385},{3... | collective-permute-start | bytes 1572872 | tf_op jit(solution)/shard_map/ppermute | solution.py:12
  118.5 12.3 %collective-permute-start.9 = (bf16[512,512]{1,0:T(8,128)(2,1)S(1)}, bf16[512,512]{1,0:T(8,128)(2,1)S(1)}, u32[]{:S(2)}, u32[]{:S(2)}) collective-permute-start(bf16[512,512]{1,0:T(8,128)(2,1)S(1)} %slice.45), channel_id=1, source_target_pairs={{0,384},{128,0},{256,128},{384,256},{1,385},{129,1},{257,129},{385... | collective-permute-start | bytes 1572872 | tf_op jit(solution)/shard_map/ppermute | solution.py:12
  125.8 5.0 %copy-start.7 = (bf16[384,512]{1,0:T(8,128)(2,1)S(1)}, bf16[384,512]{1,0:T(8,128)(2,1)}, u32[]{:S(2)}) copy-start(bf16[384,512]{1,0:T(8,128)(2,1)} %param.5) | copy-start | bytes 1179652
  125.8 5.0 %copy-start.8 = (bf16[384,512]{1,0:T(8,128)(2,1)S(1)}, bf16[384,512]{1,0:T(8,128)(2,1)}, u32[]{:S(2)}) copy-start(bf16[384,512]{1,0:T(8,128)(2,1)} %param.6) | copy-start | bytes 1179652

commit v2 on v1

--- a/solution.py
+++ b/solution.py
@@ -14,9 +14,8 @@
 
 def gather_line(x, axis, n):
     c = lax.axis_index(axis)
-    parts = [_line(x, axis, n, n - 1 - j) if j < n - 1 else x for j in range(n)]
-    parts += [_line(x, axis, n, -k) for k in range(1, n)]
-    stack = jnp.stack(parts)
+    parts = [x] + [_ring(x, axis, n, k) for k in range(1, n)]
+    stack = jnp.stack(parts[::-1] + parts[:0:-1])
     out = lax.dynamic_slice_in_dim(stack, n - 1 - c, n, axis=0)
     return out.reshape((n * x.shape[0],) + x.shape[1:])
 
@@ -34,10 +33,10 @@
     b0, b1, b2, b3 = blocks
     h = b0.shape[0] // 2
     bf = jnp.bfloat16
-    s1p = _ring(b1[h:].astype(bf), axis, 4, 1)
-    x1 = _ring(b2[:h].astype(bf), axis, 4, 1)
-    s1m = _ring(b3[:h].astype(bf), axis, 4, -1)
-    y1 = _ring(b2[h:].astype(bf), axis, 4, -1)
+    got_p = _ring(jnp.concatenate([b1[h:], b2[:h]]).astype(bf), axis, 4, 1)
+    got_m = _ring(jnp.concatenate([b3[:h], b2[h:]]).astype(bf), axis, 4, -1)
+    s1p, x1 = got_p[:h], got_p[h:]
+    s1m, y1 = got_m[:h], got_m[h:]
     s2p = _ring((b1[:h] + x1.astype(jnp.float32)).astype(bf), axis, 4, 1)
     s2m = _ring((b3[h:] + y1.astype(jnp.float32)).astype(bf), axis, 4, -1)
     f32 = jnp.float32
@@ -50,9 +49,9 @@
     c = lax.axis_index(axis)
     rows = x.shape[0] // n
     acc = lax.dynamic_slice_in_dim(x, c * rows, rows, axis=0)
-    for k in list(range(1, n)) + list(range(-n + 1, 0)):
-        part = lax.dynamic_slice_in_dim(x, jnp.clip(c + k, 0, n - 1) * rows, rows, axis=0)
-        acc = acc + _line(part.astype(jnp.bfloat16), axis, n, k).astype(jnp.float32)
+    for k in range(1, n):
+        part = lax.dynamic_slice_in_dim(x, ((c + k) % n) * rows, rows, axis=0)
+        acc = acc + _ring(part.astype(jnp.bfloat16), axis, n, k).astype(jnp.float32)
     return acc
 
 

time: 134 us -> 124 us (0.925)
  the two profiles are of different devices: /device:TPU:462 before, /device:TPU:398 now
where the time goes in v2:
time: 124 us; the launch traced here: 123 us
  starting transfers between devices  43.5 us (35%)
  waiting for transfers between devices  36.4 us (29%)
  local copies, waits for them, and re-layouts  20.4 us (16%)
  matrix products  14.5 us (12%)
  other arithmetic  7.24 us (6%)
    ppermute x14, starting transfers between devices, _ring(): return lax.ppermute(x, axis, [(i, (i + k) % n) for i in range(n)])  43.5 us
    ppermute x14, waiting for transfers between devices, _ring(): return lax.ppermute(x, axis, [(i, (i + k) % n) for i in range(n)])  36.4 us
    dot_general x4, matrix products, local(): term = jnp.dot(cols, blk, preferred_element_type=jnp.float32)  11 us
    unnamed x19, local copies, waits for them, and re-layouts  7.46 us
    dot_general x1, matrix products, local(): lax.dot_general(cotangent, hidden, (((0,), (0,)), ((), ())), preferred_el...  3.57 us
    dynamic_slice x1, local copies, waits for them, and re-layouts, local(): lax.dynamic_slice_in_dim(partial, (a + k) % ndp * span, span, axis=0)  3.18 us
  transfers between devices with their start and end apart: 14, of which 8 were waited for; matrix products, arithmetic and copies ran while one was open for 29% of the time, Pallas kernels for 0%

profile of v2, /device:TPU:398, one launch (start us, length us, event | category | flops | bytes accessed | tf_op | source)
XLA Modules:
  0.0 123.1 jit_solution(133704363722640079)
XLA Ops:
  0.6 2.6 %collective-permute-start = (bf16[256,512]{1,0:T(8,128)(2,1)}, bf16[256,512]{1,0:T(8,128)(2,1)S(1)}, u32[]{:S(2)}, u32[]{:S(2)}) collective-permute-start(bf16[256,512]{1,0:T(8,128)(2,1)} %param.7), channel_id=1, source_target_pairs={{0,96},{32,0},{64,32},{96,64},{1,97},{33,1},{65,33},{97,65},{2,98}... | collective-permute-start | bytes 786440 | tf_op jit(solution)/shard_map/ppermute | solution.py:12
  3.3 4.5 %collective-permute-start.1 = (bf16[256,512]{1,0:T(8,128)(2,1)}, bf16[256,512]{1,0:T(8,128)(2,1)}, u32[]{:S(2)}, u32[]{:S(2)}) collective-permute-start(bf16[256,512]{1,0:T(8,128)(2,1)} %param.7), channel_id=1, source_target_pairs={{0,64},{32,96},{64,0},{96,32},{1,65},{33,97},{65,1},{97,33},{2,66}... | collective-permute-start | bytes 786440 | tf_op jit(solution)/shard_map/ppermute | solution.py:12
  7.8 4.4 %collective-permute-start.2 = (bf16[256,512]{1,0:T(8,128)(2,1)}, bf16[256,512]{1,0:T(8,128)(2,1)}, u32[]{:S(2)}, u32[]{:S(2)}) collective-permute-start(bf16[256,512]{1,0:T(8,128)(2,1)} %param.7), channel_id=1, source_target_pairs={{0,32},{32,64},{64,96},{96,0},{1,33},{33,65},{65,97},{97,1},{2,34}... | collective-permute-start | bytes 786440 | tf_op jit(solution)/shard_map/ppermute | solution.py:12
  12.2 3.6 %fusion.35 = f32[512,4096]{1,0:T(8,128)S(1)} fusion(bf16[384,4096]{1,0:T(8,128)(2,1)S(1)} %copy-done, bf16[384,512]{1,0:T(8,128)(2,1)} %param.6, bf16[384,512]{1,0:T(8,128)(2,1)} %param.5), kind=kOutput, calls=%fused_computation.63 | convolution fusion | flops 1612185600 | bytes 12320768 | tf_op jit(solution)/shard_map/dot_general | solution.py:81
  15.8 3.2 %dynamic-slice_bitcast_fusion = (f32[1024,512]{0,1:T(8,128)}, f32[1024,512]{0,1:T(8,128)S(1)}, f32[1024,512]{0,1:T(8,128)}) fusion(f32[512,4096]{1,0:T(8,128)S(1)} %fusion.35, s32[]{:T(128)S(6)} %select_n.78, s32[]{:T(128)S(6)} %select_n.74, s32[]{:T(128)S(6)} %select_n.71), kind=kLoop, calls=%fused_computation.8 | loop fusion | bytes 12582924 | tf_op jit(solution)/shard_map/dynamic_slice | solution.py:84
  19.0 1.4 %copy-done.1 = f32[512,4096]{1,0:T(8,128)} copy-done((f32[512,4096]{1,0:T(8,128)}, f32[512,4096]{1,0:T(8,128)S(1)}, u32[]{:S(2)}) %copy-start.1) | copy-done | bytes 8388632
  20.4 1.3 %copy-done.4 = f32[1024,512]{0,1:T(8,128)} copy-done((f32[1024,512]{0,1:T(8,128)}, f32[1024,512]{0,1:T(8,128)S(1)}, u32[]{:S(2)}) %copy-start.4) | copy-done | bytes 2097176
  21.7 0.9 slice.93
  22.6 1.8 %fusion.1 = bf16[1024,512]{0,1:T(8,128)(2,1)S(1)} fusion(f32[512,4096]{1,0:T(8,128)} %copy-done.1, s32[]{:T(128)S(6)} %select_n.76), kind=kLoop, calls=%fused_computation.18 | loop fusion | bytes 2097156 | tf_op jit(solution)/shard_map/convert.6
  24.5 1.1 pad_maximum_fusion
  25.6 2.4 %collective-permute-start.7 = (bf16[1024,512]{0,1:T(8,128)(2,1)}, bf16[1024,512]{0,1:T(8,128)(2,1)}, u32[]{:S(2)}, u32[]{:S(2)}) collective-permute-start(bf16[1024,512]{0,1:T(8,128)(2,1)} %pad_maximum_fusion), channel_id=1, source_target_pairs={{0,128},{128,256},{256,384},{384,0},{1,129},{129,257},{257,385},{3... | collective-permute-start | bytes 3145736 | tf_op jit(solution)/shard_map/ppermute | solution.py:12
  27.9 1.3 %slice.92 = bf16[512,512]{0,1:T(8,128)(2,1)S(1)} slice(f32[1024,512]{0,1:T(8,128)} %get-tuple-element.6), slice={[0:512], [0:512]} | slice | bytes 1048576 | tf_op jit(solution)/shard_map/slice | solution.py:37
  29.2 1.1 pad_maximum_fusion.1
  30.4 3.4 %collective-permute-start.9 = (bf16[1024,512]{0,1:T(8,128)(2,1)}, bf16[1024,512]{0,1:T(8,128)(2,1)}, u32[]{:S(2)}, u32[]{:S(2)}) collective-permute-start(bf16[1024,512]{0,1:T(8,128)(2,1)} %pad_maximum_fusion.1), channel_id=1, source_target_pairs={{0,384},{128,0},{256,128},{384,256},{1,385},{129,1},{257,129},{385... | collective-permute-start | bytes 3145736 | tf_op jit(solution)/shard_map/ppermute | solution.py:12
  33.9 1.0 bitcast_dynamic-update-slice_fusion.3
  34.8 1.0 bitcast_dynamic-update-slice_fusion.1
  35.8 1.0 bitcast_dynamic-update-slice_fusion
  36.8 1.0 bitcast_dynamic-update-slice_fusion.4
  37.8 1.0 bitcast_dynamic-update-slice_fusion.2
  38.8 1.1 constant_dynamic-slice_fusion
  39.8 3.6 %collective-permute-start.4 = (bf16[1024,512]{1,0:T(8,128)(2,1)}, bf16[1024,512]{1,0:T(8,128)(2,1)}, u32[]{:S(2)}, u32[]{:S(2)}) collective-permute-start(bf16[1024,512]{1,0:T(8,128)(2,1)} %bitcast.4), channel_id=1, source_target_pairs={{0,128},{128,256},{256,384},{384,0},{1,129},{129,257},{257,385},{3... | collective-permute-start | bytes 3145736 | tf_op jit(solution)/shard_map/ppermute | solution.py:12
  43.4 2.2 %collective-permute-start.3 = (bf16[1024,512]{1,0:T(8,128)(2,1)}, bf16[1024,512]{1,0:T(8,128)(2,1)}, u32[]{:S(2)}, u32[]{:S(2)}) collective-permute-start(bf16[1024,512]{1,0:T(8,128)(2,1)} %bitcast.4), channel_id=1, source_target_pairs={{0,384},{128,0},{256,128},{384,256},{1,385},{129,1},{257,129},{385... | collective-permute-start | bytes 3145736 | tf_op jit(solution)/shard_map/ppermute | solution.py:12
  45.7 8.1 %collective-permute-done.7 = bf16[1024,512]{0,1:T(8,128)(2,1)} collective-permute-done((bf16[1024,512]{0,1:T(8,128)(2,1)}, bf16[1024,512]{0,1:T(8,128)(2,1)}, u32[]{:S(2)}, u32[]{:S(2)}) %collective-permute-start.7) | collective-permute-done | bytes 1048608 | tf_op jit(solution)/shard_map/ppermute | solution.py:12
  53.9 1.5 %fusion.4 = bf16[512,512]{0,1:T(8,128)(2,1)S(1)} fusion(f32[1024,512]{0,1:T(8,128)} %copy-done.4, bf16[1024,512]{0,1:T(8,128)(2,1)} %collective-permute-done.7), kind=kLoop, calls=%fused_computation.26 | loop fusion | flops 786432 | bytes 2097152 | tf_op jit(solution)/shard_map/convert_element_type | solution.py:40
  55.4 3.6 %collective-permute-start.8 = (bf16[512,512]{0,1:T(8,128)(2,1)S(1)}, bf16[512,512]{0,1:T(8,128)(2,1)S(1)}, u32[]{:S(2)}, u32[]{:S(2)}) collective-permute-start(bf16[512,512]{0,1:T(8,128)(2,1)S(1)} %fusion.4), channel_id=1, source_target_pairs={{0,128},{128,256},{256,384},{384,0},{1,129},{129,257},{257,385},{3... | collective-permute-start | bytes 1572872 | tf_op jit(solution)/shard_map/ppermute | solution.py:12
  59.0 0.9 collective-permute-done.9
  59.9 1.2 fusion.2
  61.1 2.2 %collective-permute-start.10 = (bf16[512,512]{0,1:T(8,128)(2,1)S(1)}, bf16[512,512]{0,1:T(8,128)(2,1)S(1)}, u32[]{:S(2)}, u32[]{:S(2)}) collective-permute-start(bf16[512,512]{0,1:T(8,128)(2,1)S(1)} %fusion.2), channel_id=1, source_target_pairs={{0,384},{128,0},{256,128},{384,256},{1,385},{129,1},{257,129},{385... | collective-permute-start | bytes 1572872 | tf_op jit(solution)/shard_map/ppermute | solution.py:12
  63.3 13.0 %collective-permute-done.4 = bf16[1024,512]{1,0:T(8,128)(2,1)} collective-permute-done((bf16[1024,512]{1,0:T(8,128)(2,1)}, bf16[1024,512]{1,0:T(8,128)(2,1)}, u32[]{:S(2)}, u32[]{:S(2)}) %collective-permute-start.4) | collective-permute-done | bytes 1048608 | tf_op jit(solution)/shard_map/ppermute | solution.py:12
  76.3 1.9 %slice.60 = bf16[512,512]{1,0:T(8,128)(2,1)} slice(bf16[1024,512]{1,0:T(8,128)(2,1)} %collective-permute-done.4), slice={[0:512], [0:512]} | slice | bytes 1048576 | tf_op jit(solution)/shard_map/slice | solution.py:27
  78.2 3.6 %collective-permute-start.5 = (bf16[512,512]{1,0:T(8,128)(2,1)}, bf16[512,512]{1,0:T(8,128)(2,1)}, u32[]{:S(2)}, u32[]{:S(2)}) collective-permute-start(bf16[512,512]{1,0:T(8,128)(2,1)} %slice.60), channel_id=1, source_target_pairs={{0,128},{128,256},{256,384},{384,0},{1,129},{129,257},{257,385},{3... | collective-permute-start | bytes 1572872 | tf_op jit(solution)/shard_map/ppermute | solution.py:12
  81.8 0.5 collective-permute-done.3
  82.3 1.9 %slice.61 = bf16[512,512]{1,0:T(8,128)(2,1)} slice(bf16[1024,512]{1,0:T(8,128)(2,1)} %collective-permute-done.3), slice={[512:1024], [0:512]} | slice | bytes 1048576 | tf_op jit(solution)/shard_map/slice | solution.py:28
  84.2 2.2 %collective-permute-start.6 = (bf16[512,512]{1,0:T(8,128)(2,1)}, bf16[512,512]{1,0:T(8,128)(2,1)}, u32[]{:S(2)}, u32[]{:S(2)}) collective-permute-start(bf16[512,512]{1,0:T(8,128)(2,1)} %slice.61), channel_id=1, source_target_pairs={{0,384},{128,0},{256,128},{384,256},{1,385},{129,1},{257,129},{385... | collective-permute-start | bytes 1572872 | tf_op jit(solution)/shard_map/ppermute | solution.py:12
  86.4 1.8 %fusion.20 = f32[384,512]{1,0:T(8,128)S(1)} fusion(bf16[1024,512]{1,0:T(8,128)(2,1)} %collective-permute-done.3, bf16[384,4096]{1,0:T(8,128)(2,1)S(1)} %copy-done, s32[]{:T(128)S(6)} %select_n.74), kind=kOutput, calls=%fused_computation.48 | convolution fusion | flops 402653184 | bytes 2621444 | tf_op jit(solution)/shard_map/dot_general | solution.py:74
  88.3 2.8 %convolution_add_fusion.1 = f32[384,512]{1,0:T(8,128)} fusion(f32[384,512]{1,0:T(8,128)S(1)} %fusion.20, bf16[1024,512]{1,0:T(8,128)(2,1)} %bitcast.4, bf16[384,4096]{1,0:T(8,128)(2,1)S(1)} %copy-done, s32[]{:T(128)S(6)} %select_n.71), kind=kOutput, calls=%fused_computation.13 | convolution fusion | flops 402849792 | bytes 3407876 | tf_op jit(solution)/shard_map/dot_general | solution.py:74
  91.1 2.4 %collective-permute-done.10 = bf16[512,512]{0,1:T(8,128)(2,1)S(1)} collective-permute-done((bf16[512,512]{0,1:T(8,128)(2,1)S(1)}, bf16[512,512]{0,1:T(8,128)(2,1)S(1)}, u32[]{:S(2)}, u32[]{:S(2)}) %collective-permute-start.10) | collective-permute-done | bytes 524320 | tf_op jit(solution)/shard_map/ppermute | solution.py:12
  93.5 1.7 %fusion.3 = (f32[512,512]{0,1:T(8,128)S(1)}, f32[512,512]{0,1:T(8,128)S(1)}) fusion(f32[1024,512]{0,1:T(8,128)S(1)} %copy-done.2, bf16[512,512]{0,1:T(8,128)(2,1)S(1)} %collective-permute-done.10, bf16[1024,512]{0,1:T(8,128)(2,1)} %collective-permute-done.7, bf16[1024,512]{0,1:T(8,128)(2,1)} %collective-permute-done.9, ...), kind=kLoop, calls=%fused_computation.22 | loop fusion | flops 2097152 | bytes 6291456 | tf_op jit(solution)/shard_map/add | solution.py:44
  95.1 0.4 fusion.32
  95.6 1.9 %collective-permute-start.11 = (bf16[256,512]{0,1:T(8,128)(2,1)S(1)}, bf16[256,512]{0,1:T(8,128)(2,1)S(1)}, u32[]{:S(2)}, u32[]{:S(2)}) collective-permute-start(bf16[256,512]{0,1:T(8,128)(2,1)S(1)} %get-tuple-element.9), channel_id=1, source_target_pairs={{0,32},{32,64},{64,96},{96,0},{1,33},{33,65},{65,97},{97,1},{2,34}... | collective-permute-start | bytes 786440 | tf_op jit(solution)/shard_map/ppermute | solution.py:12
  97.5 3.8 %collective-permute-start.12 = (bf16[256,512]{0,1:T(8,128)(2,1)S(1)}, bf16[256,512]{0,1:T(8,128)(2,1)S(1)}, u32[]{:S(2)}, u32[]{:S(2)}) collective-permute-start(bf16[256,512]{0,1:T(8,128)(2,1)S(1)} %get-tuple-element.10), channel_id=1, source_target_pairs={{0,64},{32,96},{64,0},{96,32},{1,65},{33,97},{65,1},{97,33},{2,66}... | collective-permute-start | bytes 786440 | tf_op jit(solution)/shard_map/ppermute | solution.py:12
  101.3 2.9 %collective-permute-start.13 = (bf16[256,512]{0,1:T(8,128)(2,1)S(1)}, bf16[256,512]{0,1:T(8,128)(2,1)S(1)}, u32[]{:S(2)}, u32[]{:S(2)}) collective-permute-start(bf16[256,512]{0,1:T(8,128)(2,1)S(1)} %get-tuple-element.11), channel_id=1, source_target_pairs={{0,96},{32,0},{64,32},{96,64},{1,97},{33,1},{65,33},{97,65},{2,98}... | collective-permute-start | bytes 786440 | tf_op jit(solution)/shard_map/ppermute | solution.py:12
  104.3 2.7 %fusion.17 = f32[384,512]{1,0:T(8,128)} fusion(bf16[1024,512]{1,0:T(8,128)(2,1)} %collective-permute-done.4, bf16[384,4096]{1,0:T(8,128)(2,1)S(1)} %copy-done, s32[]{:T(128)S(6)} %select_n.78), kind=kOutput, calls=%fused_computation.45 | convolution fusion | flops 402653184 | bytes 2621444 | tf_op jit(solution)/shard_map/dot_general | solution.py:74
  107.0 6.5 %collective-permute-done.11 = bf16[256,512]{0,1:T(8,128)(2,1)S(1)} collective-permute-done((bf16[256,512]{0,1:T(8,128)(2,1)S(1)}, bf16[256,512]{0,1:T(8,128)(2,1)S(1)}, u32[]{:S(2)}, u32[]{:S(2)}) %collective-permute-start.11) | collective-permute-done | bytes 262176 | tf_op jit(solution)/shard_map/ppermute | solution.py:12
  113.5 2.8 %collective-permute-done.12 = bf16[256,512]{0,1:T(8,128)(2,1)S(1)} collective-permute-done((bf16[256,512]{0,1:T(8,128)(2,1)S(1)}, bf16[256,512]{0,1:T(8,128)(2,1)S(1)}, u32[]{:S(2)}, u32[]{:S(2)}) %collective-permute-start.12) | collective-permute-done | bytes 262176 | tf_op jit(solution)/shard_map/ppermute | solution.py:12
  116.3 2.1 %collective-permute-done.13 = bf16[256,512]{0,1:T(8,128)(2,1)S(1)} collective-permute-done((bf16[256,512]{0,1:T(8,128)(2,1)S(1)}, bf16[256,512]{0,1:T(8,128)(2,1)S(1)}, u32[]{:S(2)}, u32[]{:S(2)}) %collective-permute-start.13) | collective-permute-done | bytes 262176 | tf_op jit(solution)/shard_map/ppermute | solution.py:12
  118.6 0.8 copy.7
  119.5 3.7 %multiply_convert_fusion = (bf16[384,512]{1,0:T(8,128)(2,1)}, bf16[384,512]{1,0:T(8,128)(2,1)}) fusion(bf16[384,512]{1,0:T(8,128)(2,1)} %param.5, bf16[384,512]{1,0:T(8,128)(2,1)} %param.6, f32[384,512]{1,0:T(8,128)} %fusion.17, f32[384,512]{1,0:T(8,128)} %convolution_add_fusion.1, bf16[512,512]{1,0:T(8,128)(2,1)} %collective-permute-done.6, ...), kind=kOutput, calls=%fused_computation.44 | convolution fusion | flops 408092672 | bytes 4980740 | tf_op jit(solution)/shard_map/dot_general | solution.py:74
  (20 shorter events, 0.4 us)
Async XLA Ops:
  0.6 11.6 %copy-start = (bf16[384,4096]{1,0:T(8,128)(2,1)S(1)}, bf16[384,4096]{1,0:T(8,128)(2,1)}, u32[]{:S(2)}) copy-start(bf16[384,4096]{1,0:T(8,128)(2,1)} %param.4) | copy-start | bytes 9437188
  0.6 33.2 %collective-permute-start = (bf16[256,512]{1,0:T(8,128)(2,1)}, bf16[256,512]{1,0:T(8,128)(2,1)S(1)}, u32[]{:S(2)}, u32[]{:S(2)}) collective-permute-start(bf16[256,512]{1,0:T(8,128)(2,1)} %param.7), channel_id=1, source_target_pairs={{0,96},{32,0},{64,32},{96,64},{1,97},{33,1},{65,33},{97,65},{2,98}... | collective-permute-start | bytes 786440 | tf_op jit(solution)/shard_map/ppermute | solution.py:12
  3.3 30.6 %collective-permute-start.1 = (bf16[256,512]{1,0:T(8,128)(2,1)}, bf16[256,512]{1,0:T(8,128)(2,1)}, u32[]{:S(2)}, u32[]{:S(2)}) collective-permute-start(bf16[256,512]{1,0:T(8,128)(2,1)} %param.7), channel_id=1, source_target_pairs={{0,64},{32,96},{64,0},{96,32},{1,65},{33,97},{65,1},{97,33},{2,66}... | collective-permute-start | bytes 786440 | tf_op jit(solution)/shard_map/ppermute | solution.py:12
  7.8 27.1 %collective-permute-start.2 = (bf16[256,512]{1,0:T(8,128)(2,1)}, bf16[256,512]{1,0:T(8,128)(2,1)}, u32[]{:S(2)}, u32[]{:S(2)}) collective-permute-start(bf16[256,512]{1,0:T(8,128)(2,1)} %param.7), channel_id=1, source_target_pairs={{0,32},{32,64},{64,96},{96,0},{1,33},{33,65},{65,97},{97,1},{2,34}... | collective-permute-start | bytes 786440 | tf_op jit(solution)/shard_map/ppermute | solution.py:12
  15.8 4.6 %copy-start.1 = (f32[512,4096]{1,0:T(8,128)}, f32[512,4096]{1,0:T(8,128)S(1)}, u32[]{:S(2)}) copy-start(f32[512,4096]{1,0:T(8,128)S(1)} %fusion.35) | copy-start | bytes 25165828
  20.4 1.3 %copy-start.4 = (f32[1024,512]{0,1:T(8,128)}, f32[1024,512]{0,1:T(8,128)S(1)}, u32[]{:S(2)}) copy-start(f32[1024,512]{0,1:T(8,128)S(1)} %get-tuple-element.7) | copy-start | bytes 6291460
  22.6 1.9 %copy-start.5 = (bf16[512,512]{0,1:T(8,128)(2,1)S(1)}, bf16[512,512]{0,1:T(8,128)(2,1)}, u32[]{:S(2)}) copy-start(bf16[512,512]{0,1:T(8,128)(2,1)} %slice.93) | copy-start | bytes 1572868
  25.6 28.3 %collective-permute-start.7 = (bf16[1024,512]{0,1:T(8,128)(2,1)}, bf16[1024,512]{0,1:T(8,128)(2,1)}, u32[]{:S(2)}, u32[]{:S(2)}) collective-permute-start(bf16[1024,512]{0,1:T(8,128)(2,1)} %pad_maximum_fusion), channel_id=1, source_target_pairs={{0,128},{128,256},{256,384},{384,0},{1,129},{129,257},{257,385},{3... | collective-permute-start | bytes 3145736 | tf_op jit(solution)/shard_map/ppermute | solution.py:12
  30.4 29.5 %collective-permute-start.9 = (bf16[1024,512]{0,1:T(8,128)(2,1)}, bf16[1024,512]{0,1:T(8,128)(2,1)}, u32[]{:S(2)}, u32[]{:S(2)}) collective-permute-start(bf16[1024,512]{0,1:T(8,128)(2,1)} %pad_maximum_fusion.1), channel_id=1, source_target_pairs={{0,384},{128,0},{256,128},{384,256},{1,385},{129,1},{257,129},{385... | collective-permute-start | bytes 3145736 | tf_op jit(solution)/shard_map/ppermute | solution.py:12
  39.8 36.5 %collective-permute-start.4 = (bf16[1024,512]{1,0:T(8,128)(2,1)}, bf16[1024,512]{1,0:T(8,128)(2,1)}, u32[]{:S(2)}, u32[]{:S(2)}) collective-permute-start(bf16[1024,512]{1,0:T(8,128)(2,1)} %bitcast.4), channel_id=1, source_target_pairs={{0,128},{128,256},{256,384},{384,0},{1,129},{129,257},{257,385},{3... | collective-permute-start | bytes 3145736 | tf_op jit(solution)/shard_map/ppermute | solution.py:12
  43.4 38.9 %collective-permute-start.3 = (bf16[1024,512]{1,0:T(8,128)(2,1)}, bf16[1024,512]{1,0:T(8,128)(2,1)}, u32[]{:S(2)}, u32[]{:S(2)}) collective-permute-start(bf16[1024,512]{1,0:T(8,128)(2,1)} %bitcast.4), channel_id=1, source_target_pairs={{0,384},{128,0},{256,128},{384,256},{1,385},{129,1},{257,129},{385... | collective-permute-start | bytes 3145736 | tf_op jit(solution)/shard_map/ppermute | solution.py:12
  45.7 14.2 %copy-start.3 = (f32[1024,512]{0,1:T(8,128)S(1)}, f32[1024,512]{0,1:T(8,128)}, u32[]{:S(2)}) copy-start(f32[1024,512]{0,1:T(8,128)} %get-tuple-element.6) | copy-start | bytes 6291460
  55.4 35.7 %collective-permute-start.8 = (bf16[512,512]{0,1:T(8,128)(2,1)S(1)}, bf16[512,512]{0,1:T(8,128)(2,1)S(1)}, u32[]{:S(2)}, u32[]{:S(2)}) collective-permute-start(bf16[512,512]{0,1:T(8,128)(2,1)S(1)} %fusion.4), channel_id=1, source_target_pairs={{0,128},{128,256},{256,384},{384,0},{1,129},{129,257},{257,385},{3... | collective-permute-start | bytes 1572872 | tf_op jit(solution)/shard_map/ppermute | solution.py:12
  61.1 32.4 %collective-permute-start.10 = (bf16[512,512]{0,1:T(8,128)(2,1)S(1)}, bf16[512,512]{0,1:T(8,128)(2,1)S(1)}, u32[]{:S(2)}, u32[]{:S(2)}) collective-permute-start(bf16[512,512]{0,1:T(8,128)(2,1)S(1)} %fusion.2), channel_id=1, source_target_pairs={{0,384},{128,0},{256,128},{384,256},{1,385},{129,1},{257,129},{385... | collective-permute-start | bytes 1572872 | tf_op jit(solution)/shard_map/ppermute | solution.py:12
  78.2 41.2 %collective-permute-start.5 = (bf16[512,512]{1,0:T(8,128)(2,1)}, bf16[512,512]{1,0:T(8,128)(2,1)}, u32[]{:S(2)}, u32[]{:S(2)}) collective-permute-start(bf16[512,512]{1,0:T(8,128)(2,1)} %slice.60), channel_id=1, source_target_pairs={{0,128},{128,256},{256,384},{384,0},{1,129},{129,257},{257,385},{3... | collective-permute-start | bytes 1572872 | tf_op jit(solution)/shard_map/ppermute | solution.py:12
  84.2 35.3 %collective-permute-start.6 = (bf16[512,512]{1,0:T(8,128)(2,1)}, bf16[512,512]{1,0:T(8,128)(2,1)}, u32[]{:S(2)}, u32[]{:S(2)}) collective-permute-start(bf16[512,512]{1,0:T(8,128)(2,1)} %slice.61), channel_id=1, source_target_pairs={{0,384},{128,0},{256,128},{384,256},{1,385},{129,1},{257,129},{385... | collective-permute-start | bytes 1572872 | tf_op jit(solution)/shard_map/ppermute | solution.py:12
  88.2 5.2 %copy-start.2 = (f32[1024,512]{0,1:T(8,128)S(1)}, f32[1024,512]{0,1:T(8,128)}, u32[]{:S(2)}) copy-start(f32[1024,512]{0,1:T(8,128)} %get-tuple-element.8) | copy-start | bytes 6291460
  95.6 17.9 %collective-permute-start.11 = (bf16[256,512]{0,1:T(8,128)(2,1)S(1)}, bf16[256,512]{0,1:T(8,128)(2,1)S(1)}, u32[]{:S(2)}, u32[]{:S(2)}) collective-permute-start(bf16[256,512]{0,1:T(8,128)(2,1)S(1)} %get-tuple-element.9), channel_id=1, source_target_pairs={{0,32},{32,64},{64,96},{96,0},{1,33},{33,65},{65,97},{97,1},{2,34}... | collective-permute-start | bytes 786440 | tf_op jit(solution)/shard_map/ppermute | solution.py:12
  97.5 18.8 %collective-permute-start.12 = (bf16[256,512]{0,1:T(8,128)(2,1)S(1)}, bf16[256,512]{0,1:T(8,128)(2,1)S(1)}, u32[]{:S(2)}, u32[]{:S(2)}) collective-permute-start(bf16[256,512]{0,1:T(8,128)(2,1)S(1)} %get-tuple-element.10), channel_id=1, source_target_pairs={{0,64},{32,96},{64,0},{96,32},{1,65},{33,97},{65,1},{97,33},{2,66}... | collective-permute-start | bytes 786440 | tf_op jit(solution)/shard_map/ppermute | solution.py:12
  101.3 17.1 %collective-permute-start.13 = (bf16[256,512]{0,1:T(8,128)(2,1)S(1)}, bf16[256,512]{0,1:T(8,128)(2,1)S(1)}, u32[]{:S(2)}, u32[]{:S(2)}) collective-permute-start(bf16[256,512]{0,1:T(8,128)(2,1)S(1)} %get-tuple-element.11), channel_id=1, source_target_pairs={{0,96},{32,0},{64,32},{96,64},{1,97},{33,1},{65,33},{97,65},{2,98}... | collective-permute-start | bytes 786440 | tf_op jit(solution)/shard_map/ppermute | solution.py:12

commit v3 on v2

--- a/solution.py
+++ b/solution.py
@@ -66,6 +66,14 @@
     groups = ndp * nctx
     a = lax.axis_index("dp")
 
+    span_rs = w_down.shape[0] * nctx
+    partial = lax.dot_general(
+        cotangent, hidden, (((0,), (0,)), ((), ())), preferred_element_type=jnp.float32
+    )
+    blocks = [lax.dynamic_slice_in_dim(partial, ((a + k) % ndp) * span_rs, span_rs, axis=0) for k in range(4)]
+    w_down, blocks = lax.optimization_barrier((w_down, blocks))
+    reduced = scatter_ring4(blocks, "dp")
+    summed = scatter_line(reduced, "ctx", nctx)
     w_ctx = gather_line(w_down, "ctx", nctx)
     span = w_ctx.shape[0]
     grad_hidden = None
@@ -78,12 +86,6 @@
     ).astype(jnp.bfloat16)
     grad_up = (grad_hidden * activated).astype(jnp.bfloat16)
 
-    partial = lax.dot_general(
-        cotangent, hidden, (((0,), (0,)), ((), ())), preferred_element_type=jnp.float32
-    )
-    blocks = [lax.dynamic_slice_in_dim(partial, ((a + k) % ndp) * span, span, axis=0) for k in range(4)]
-    reduced = scatter_ring4(blocks, "dp")
-    summed = scatter_line(reduced, "ctx", nctx)
     grad_down = (summed / groups).astype(jnp.bfloat16)
     return (grad_gate, grad_up, grad_down)
 

time: 124 us -> 120 us (0.968)
  the two profiles are of different devices: /device:TPU:398 before, /device:TPU:8 now
where the time goes in v3:
time: 120 us; the launch traced here: 119 us
  starting transfers between devices  52.4 us (44%)
  waiting for transfers between devices  29 us (24%)
  local copies, waits for them, and re-layouts  15 us (12%)
  matrix products  14.5 us (12%)
  other arithmetic  7.32 us (6%)
    ppermute x14, starting transfers between devices, _ring(): return lax.ppermute(x, axis, [(i, (i + k) % n) for i in range(n)])  52.4 us
    ppermute x14, waiting for transfers between devices, _ring(): return lax.ppermute(x, axis, [(i, (i + k) % n) for i in range(n)])  29 us
    dot_general x4, matrix products, local(): term = jnp.dot(cols, blk, preferred_element_type=jnp.float32)  11 us
    unnamed x17, local copies, waits for them, and re-layouts  6.6 us
    dot_general x1, matrix products, local(): lax.dot_general(cotangent, hidden, (((0,), (0,)), ((), ())), preferred_el...  3.57 us
    dynamic_slice x2, local copies, waits for them, and re-layouts, local(): lax.dynamic_slice_in_dim(partial, (a + k) % ndp * span_rs, span_rs, axis=0)  2.44 us
  transfers between devices with their start and end apart: 14, of which 8 were waited for; matrix products, arithmetic and copies ran while one was open for 21% of the time, Pallas kernels for 0%

profile of v3, /device:TPU:8, one launch (start us, length us, event | category | flops | bytes accessed | tf_op | source)
XLA Modules:
  0.0 119.3 jit_solution(6835499375194017316)
XLA Ops:
  0.7 1.8 %copy-done = bf16[384,4096]{1,0:T(8,128)(2,1)S(1)} copy-done((bf16[384,4096]{1,0:T(8,128)(2,1)S(1)}, bf16[384,4096]{1,0:T(8,128)(2,1)}, u32[]{:S(2)}) %copy-start) | copy-done | bytes 3145752
  2.5 3.6 %fusion.30 = f32[512,4096]{1,0:T(8,128)S(1)} fusion(bf16[384,4096]{1,0:T(8,128)(2,1)S(1)} %copy-done, bf16[384,512]{1,0:T(8,128)(2,1)} %param.6, bf16[384,512]{1,0:T(8,128)(2,1)} %param.5), kind=kOutput, calls=%fused_computation.58 | convolution fusion | flops 1612185600 | bytes 12320768 | tf_op jit(solution)/shard_map/dot_general | solution.py:70
  6.1 0.2 dynamic-slice_bitcast_fusion.1
  6.3 2.3 %dynamic-slice_bitcast_fusion = (f32[1024,512]{0,1:T(8,128)S(1)}, f32[1024,512]{0,1:T(8,128)S(1)}, f32[1024,512]{0,1:T(8,128)}) fusion(f32[512,4096]{1,0:T(8,128)S(1)} %fusion.30, s32[]{:T(128)S(6)} %select_n.77, s32[]{:T(128)S(6)} %select_n.73, s32[]{:T(128)S(6)} %select_n.71), kind=kLoop, calls=%fused_computation.8 | loop fusion | bytes 12582924 | tf_op jit(solution)/shard_map/dynamic_slice | solution.py:73
  8.5 7.7 %collective-permute-start = (bf16[256,512]{1,0:T(8,128)(2,1)}, bf16[256,512]{1,0:T(8,128)(2,1)S(1)}, u32[]{:S(2)}, u32[]{:S(2)}) collective-permute-start(bf16[256,512]{1,0:T(8,128)(2,1)} %param.7), channel_id=1, source_target_pairs={{0,96},{32,0},{64,32},{96,64},{1,97},{33,1},{65,33},{97,65},{2,98}... | collective-permute-start | bytes 786440 | tf_op jit(solution)/shard_map/ppermute | solution.py:12
  16.3 1.9 %collective-permute-start.1 = (bf16[256,512]{1,0:T(8,128)(2,1)}, bf16[256,512]{1,0:T(8,128)(2,1)}, u32[]{:S(2)}, u32[]{:S(2)}) collective-permute-start(bf16[256,512]{1,0:T(8,128)(2,1)} %param.7), channel_id=1, source_target_pairs={{0,64},{32,96},{64,0},{96,32},{1,65},{33,97},{65,1},{97,33},{2,66}... | collective-permute-start | bytes 786440 | tf_op jit(solution)/shard_map/ppermute | solution.py:12
  18.2 3.4 %collective-permute-start.2 = (bf16[256,512]{1,0:T(8,128)(2,1)}, bf16[256,512]{1,0:T(8,128)(2,1)}, u32[]{:S(2)}, u32[]{:S(2)}) collective-permute-start(bf16[256,512]{1,0:T(8,128)(2,1)} %param.7), channel_id=1, source_target_pairs={{0,32},{32,64},{64,96},{96,0},{1,33},{33,65},{65,97},{97,1},{2,34}... | collective-permute-start | bytes 786440 | tf_op jit(solution)/shard_map/ppermute | solution.py:12
  21.7 0.1 slice.81
  21.7 1.2 pad_maximum_fusion
  22.9 1.9 %collective-permute-start.7 = (bf16[1024,512]{0,1:T(8,128)(2,1)}, bf16[1024,512]{0,1:T(8,128)(2,1)}, u32[]{:S(2)}, u32[]{:S(2)}) collective-permute-start(bf16[1024,512]{0,1:T(8,128)(2,1)} %pad_maximum_fusion), channel_id=1, source_target_pairs={{0,128},{128,256},{256,384},{384,0},{1,129},{129,257},{257,385},{3... | collective-permute-start | bytes 3145736 | tf_op jit(solution)/shard_map/ppermute | solution.py:12
  24.8 0.1 slice.80
  24.9 1.1 pad_maximum_fusion.1
  26.0 5.1 %collective-permute-start.9 = (bf16[1024,512]{0,1:T(8,128)(2,1)}, bf16[1024,512]{0,1:T(8,128)(2,1)}, u32[]{:S(2)}, u32[]{:S(2)}) collective-permute-start(bf16[1024,512]{0,1:T(8,128)(2,1)} %pad_maximum_fusion.1), channel_id=1, source_target_pairs={{0,384},{128,0},{256,128},{384,256},{1,385},{129,1},{257,129},{385... | collective-permute-start | bytes 3145736 | tf_op jit(solution)/shard_map/ppermute | solution.py:12
  31.2 1.0 bitcast_dynamic-update-slice_fusion.3
  32.2 4.5 %collective-permute-done.2 = bf16[256,512]{1,0:T(8,128)(2,1)} collective-permute-done((bf16[256,512]{1,0:T(8,128)(2,1)}, bf16[256,512]{1,0:T(8,128)(2,1)}, u32[]{:S(2)}, u32[]{:S(2)}) %collective-permute-start.2) | collective-permute-done | bytes 262176 | tf_op jit(solution)/shard_map/ppermute | solution.py:12
  36.7 1.0 bitcast_dynamic-update-slice_fusion.1
  37.6 1.0 bitcast_dynamic-update-slice_fusion
  38.6 1.0 bitcast_dynamic-update-slice_fusion.4
  39.6 1.0 bitcast_dynamic-update-slice_fusion.2
  40.6 1.1 constant_dynamic-slice_fusion
  41.6 3.4 %collective-permute-start.4 = (bf16[1024,512]{1,0:T(8,128)(2,1)}, bf16[1024,512]{1,0:T(8,128)(2,1)}, u32[]{:S(2)}, u32[]{:S(2)}) collective-permute-start(bf16[1024,512]{1,0:T(8,128)(2,1)} %bitcast.8), channel_id=1, source_target_pairs={{0,128},{128,256},{256,384},{384,0},{1,129},{129,257},{257,385},{3... | collective-permute-start | bytes 3145736 | tf_op jit(solution)/shard_map/ppermute | solution.py:12
  45.0 3.7 %collective-permute-start.3 = (bf16[1024,512]{1,0:T(8,128)(2,1)}, bf16[1024,512]{1,0:T(8,128)(2,1)}, u32[]{:S(2)}, u32[]{:S(2)}) collective-permute-start(bf16[1024,512]{1,0:T(8,128)(2,1)} %bitcast.8), channel_id=1, source_target_pairs={{0,384},{128,0},{256,128},{384,256},{1,385},{129,1},{257,129},{385... | collective-permute-start | bytes 3145736 | tf_op jit(solution)/shard_map/ppermute | solution.py:12
  48.8 0.7 collective-permute-done.7
  49.5 1.5 %add_convert_fusion.1 = bf16[512,512]{0,1:T(8,128)(2,1)S(1)} fusion(f32[1024,512]{0,1:T(8,128)} %copy-done.4, bf16[1024,512]{0,1:T(8,128)(2,1)} %collective-permute-done.7), kind=kLoop, calls=%fused_computation.28 | loop fusion | flops 786432 | bytes 2097152 | tf_op jit(solution)/shard_map/convert_element_type | solution.py:40
  51.0 2.2 %collective-permute-start.8 = (bf16[512,512]{0,1:T(8,128)(2,1)S(1)}, bf16[512,512]{0,1:T(8,128)(2,1)S(1)}, u32[]{:S(2)}, u32[]{:S(2)}) collective-permute-start(bf16[512,512]{0,1:T(8,128)(2,1)S(1)} %add_convert_fusion.1), channel_id=1, source_target_pairs={{0,128},{128,256},{256,384},{384,0},{1,129},{129,257},{257,385},{3... | collective-permute-start | bytes 1572872 | tf_op jit(solution)/shard_map/ppermute | solution.py:12
  53.2 0.6 collective-permute-done.9
  53.8 1.2 %add_convert_fusion = bf16[512,512]{0,1:T(8,128)(2,1)S(1)} fusion(f32[1024,512]{0,1:T(8,128)S(1)} %copy-done.3, bf16[1024,512]{0,1:T(8,128)(2,1)} %collective-permute-done.9), kind=kLoop, calls=%fused_computation.26 | loop fusion | flops 786432 | bytes 2097152 | tf_op jit(solution)/shard_map/convert_element_type | solution.py:41
  55.0 4.9 %collective-permute-start.10 = (bf16[512,512]{0,1:T(8,128)(2,1)S(1)}, bf16[512,512]{0,1:T(8,128)(2,1)S(1)}, u32[]{:S(2)}, u32[]{:S(2)}) collective-permute-start(bf16[512,512]{0,1:T(8,128)(2,1)S(1)} %add_convert_fusion), channel_id=1, source_target_pairs={{0,384},{128,0},{256,128},{384,256},{1,385},{129,1},{257,129},{385... | collective-permute-start | bytes 1572872 | tf_op jit(solution)/shard_map/ppermute | solution.py:12
  59.9 12.1 %collective-permute-done.4 = bf16[1024,512]{1,0:T(8,128)(2,1)} collective-permute-done((bf16[1024,512]{1,0:T(8,128)(2,1)}, bf16[1024,512]{1,0:T(8,128)(2,1)}, u32[]{:S(2)}, u32[]{:S(2)}) %collective-permute-start.4) | collective-permute-done | bytes 1048608 | tf_op jit(solution)/shard_map/ppermute | solution.py:12
  71.9 1.9 %slice.60 = bf16[512,512]{1,0:T(8,128)(2,1)} slice(bf16[1024,512]{1,0:T(8,128)(2,1)} %collective-permute-done.4), slice={[0:512], [0:512]} | slice | bytes 1048576 | tf_op jit(solution)/shard_map/slice | solution.py:27
  73.8 2.2 %collective-permute-start.5 = (bf16[512,512]{1,0:T(8,128)(2,1)}, bf16[512,512]{1,0:T(8,128)(2,1)}, u32[]{:S(2)}, u32[]{:S(2)}) collective-permute-start(bf16[512,512]{1,0:T(8,128)(2,1)} %slice.60), channel_id=1, source_target_pairs={{0,128},{128,256},{256,384},{384,0},{1,129},{129,257},{257,385},{3... | collective-permute-start | bytes 1572872 | tf_op jit(solution)/shard_map/ppermute | solution.py:12
  76.0 0.3 collective-permute-done.3
  76.2 1.9 %slice.61 = bf16[512,512]{1,0:T(8,128)(2,1)} slice(bf16[1024,512]{1,0:T(8,128)(2,1)} %collective-permute-done.3), slice={[512:1024], [0:512]} | slice | bytes 1048576 | tf_op jit(solution)/shard_map/slice | solution.py:28
  78.1 4.9 %collective-permute-start.6 = (bf16[512,512]{1,0:T(8,128)(2,1)}, bf16[512,512]{1,0:T(8,128)(2,1)}, u32[]{:S(2)}, u32[]{:S(2)}) collective-permute-start(bf16[512,512]{1,0:T(8,128)(2,1)} %slice.61), channel_id=1, source_target_pairs={{0,384},{128,0},{256,128},{384,256},{1,385},{129,1},{257,129},{385... | collective-permute-start | bytes 1572872 | tf_op jit(solution)/shard_map/ppermute | solution.py:12
  83.0 1.8 %fusion.15 = f32[384,512]{1,0:T(8,128)S(1)} fusion(bf16[1024,512]{1,0:T(8,128)(2,1)} %collective-permute-done.3, bf16[384,4096]{1,0:T(8,128)(2,1)S(1)} %copy-done, s32[]{:T(128)S(6)} %select_n.73), kind=kOutput, calls=%fused_computation.43 | convolution fusion | flops 402653184 | bytes 2621444 | tf_op jit(solution)/shard_map/dot_general | solution.py:82
  84.8 2.8 %convolution_add_fusion.1 = f32[384,512]{1,0:T(8,128)} fusion(f32[384,512]{1,0:T(8,128)S(1)} %fusion.15, bf16[1024,512]{1,0:T(8,128)(2,1)} %bitcast.8, bf16[384,4096]{1,0:T(8,128)(2,1)S(1)} %copy-done, s32[]{:T(128)S(6)} %select_n.71), kind=kOutput, calls=%fused_computation.13 | convolution fusion | flops 402849792 | bytes 3407876 | tf_op jit(solution)/shard_map/dot_general | solution.py:82
  87.6 1.7 %convert_add_fusion = (f32[512,512]{0,1:T(8,128)S(1)}, f32[512,512]{0,1:T(8,128)S(1)}) fusion(bf16[512,512]{0,1:T(8,128)(2,1)S(1)} %collective-permute-done.10, f32[1024,512]{0,1:T(8,128)S(1)} %copy-done.1, bf16[1024,512]{0,1:T(8,128)(2,1)} %collective-permute-done.7, bf16[1024,512]{0,1:T(8,128)(2,1)} %collective-permute-done.9, ...), kind=kLoop, calls=%fused_computation.25 | loop fusion | flops 2097152 | bytes 6291456 | tf_op jit(solution)/shard_map/add | solution.py:44
  89.3 0.4 fusion.27
  89.8 3.3 %collective-permute-start.11 = (bf16[256,512]{0,1:T(8,128)(2,1)S(1)}, bf16[256,512]{0,1:T(8,128)(2,1)S(1)}, u32[]{:S(2)}, u32[]{:S(2)}) collective-permute-start(bf16[256,512]{0,1:T(8,128)(2,1)S(1)} %get-tuple-element.19), channel_id=1, source_target_pairs={{0,32},{32,64},{64,96},{96,0},{1,33},{33,65},{65,97},{97,1},{2,34}... | collective-permute-start | bytes 786440 | tf_op jit(solution)/shard_map/ppermute | solution.py:12
  93.1 4.0 %collective-permute-start.12 = (bf16[256,512]{0,1:T(8,128)(2,1)S(1)}, bf16[256,512]{0,1:T(8,128)(2,1)S(1)}, u32[]{:S(2)}, u32[]{:S(2)}) collective-permute-start(bf16[256,512]{0,1:T(8,128)(2,1)S(1)} %get-tuple-element.20), channel_id=1, source_target_pairs={{0,64},{32,96},{64,0},{96,32},{1,65},{33,97},{65,1},{97,33},{2,66}... | collective-permute-start | bytes 786440 | tf_op jit(solution)/shard_map/ppermute | solution.py:12
  97.1 3.9 %collective-permute-start.13 = (bf16[256,512]{0,1:T(8,128)(2,1)S(1)}, bf16[256,512]{0,1:T(8,128)(2,1)S(1)}, u32[]{:S(2)}, u32[]{:S(2)}) collective-permute-start(bf16[256,512]{0,1:T(8,128)(2,1)S(1)} %get-tuple-element.21), channel_id=1, source_target_pairs={{0,96},{32,0},{64,32},{96,64},{1,97},{33,1},{65,33},{97,65},{2,98}... | collective-permute-start | bytes 786440 | tf_op jit(solution)/shard_map/ppermute | solution.py:12
  101.0 2.7 %fusion.12 = f32[384,512]{1,0:T(8,128)} fusion(bf16[1024,512]{1,0:T(8,128)(2,1)} %collective-permute-done.4, bf16[384,4096]{1,0:T(8,128)(2,1)S(1)} %copy-done, s32[]{:T(128)S(6)} %select_n.77), kind=kOutput, calls=%fused_computation.40 | convolution fusion | flops 402653184 | bytes 2621444 | tf_op jit(solution)/shard_map/dot_general | solution.py:82
  103.7 6.8 %collective-permute-done.11 = bf16[256,512]{0,1:T(8,128)(2,1)S(1)} collective-permute-done((bf16[256,512]{0,1:T(8,128)(2,1)S(1)}, bf16[256,512]{0,1:T(8,128)(2,1)S(1)}, u32[]{:S(2)}, u32[]{:S(2)}) %collective-permute-start.11) | collective-permute-done | bytes 262176 | tf_op jit(solution)/shard_map/ppermute | solution.py:12
  110.5 2.8 %collective-permute-done.12 = bf16[256,512]{0,1:T(8,128)(2,1)S(1)} collective-permute-done((bf16[256,512]{0,1:T(8,128)(2,1)S(1)}, bf16[256,512]{0,1:T(8,128)(2,1)S(1)}, u32[]{:S(2)}, u32[]{:S(2)}) %collective-permute-start.12) | collective-permute-done | bytes 262176 | tf_op jit(solution)/shard_map/ppermute | solution.py:12
  113.3 1.3 %collective-permute-done.13 = bf16[256,512]{0,1:T(8,128)(2,1)S(1)} collective-permute-done((bf16[256,512]{0,1:T(8,128)(2,1)S(1)}, bf16[256,512]{0,1:T(8,128)(2,1)S(1)}, u32[]{:S(2)}, u32[]{:S(2)}) %collective-permute-start.13) | collective-permute-done | bytes 262176 | tf_op jit(solution)/shard_map/ppermute | solution.py:12
  114.6 0.2 fusion.25
  114.8 0.8 copy.7
  115.7 3.7 %multiply_convert_fusion = (bf16[384,512]{1,0:T(8,128)(2,1)}, bf16[384,512]{1,0:T(8,128)(2,1)}) fusion(bf16[384,512]{1,0:T(8,128)(2,1)} %param.5, bf16[384,512]{1,0:T(8,128)(2,1)} %param.6, f32[384,512]{1,0:T(8,128)} %fusion.12, f32[384,512]{1,0:T(8,128)} %convolution_add_fusion.1, bf16[512,512]{1,0:T(8,128)(2,1)} %collective-permute-done.6, ...), kind=kOutput, calls=%fused_computation.39 | convolution fusion | flops 408092672 | bytes 4980740 | tf_op jit(solution)/shard_map/dot_general | solution.py:82
  (18 shorter events, 0.1 us)
Async XLA Ops:
  0.6 1.9 %copy-start = (bf16[384,4096]{1,0:T(8,128)(2,1)S(1)}, bf16[384,4096]{1,0:T(8,128)(2,1)}, u32[]{:S(2)}) copy-start(bf16[384,4096]{1,0:T(8,128)(2,1)} %param.4) | copy-start | bytes 9437188
  8.5 14.4 %copy-start.4 = (f32[1024,512]{0,1:T(8,128)}, f32[1024,512]{0,1:T(8,128)S(1)}, u32[]{:S(2)}) copy-start(f32[1024,512]{0,1:T(8,128)S(1)} %get-tuple-element.10) | copy-start | bytes 6291460
  8.5 16.3 %copy-start.2 = (f32[1024,512]{0,1:T(8,128)}, f32[1024,512]{0,1:T(8,128)S(1)}, u32[]{:S(2)}) copy-start(f32[1024,512]{0,1:T(8,128)S(1)} %get-tuple-element.12) | copy-start | bytes 6291460
  8.5 22.6 %collective-permute-start = (bf16[256,512]{1,0:T(8,128)(2,1)}, bf16[256,512]{1,0:T(8,128)(2,1)S(1)}, u32[]{:S(2)}, u32[]{:S(2)}) collective-permute-start(bf16[256,512]{1,0:T(8,128)(2,1)} %param.7), channel_id=1, source_target_pairs={{0,96},{32,0},{64,32},{96,64},{1,97},{33,1},{65,33},{97,65},{2,98}... | collective-permute-start | bytes 786440 | tf_op jit(solution)/shard_map/ppermute | solution.py:12
  16.3 14.9 %collective-permute-start.1 = (bf16[256,512]{1,0:T(8,128)(2,1)}, bf16[256,512]{1,0:T(8,128)(2,1)}, u32[]{:S(2)}, u32[]{:S(2)}) collective-permute-start(bf16[256,512]{1,0:T(8,128)(2,1)} %param.7), channel_id=1, source_target_pairs={{0,64},{32,96},{64,0},{96,32},{1,65},{33,97},{65,1},{97,33},{2,66}... | collective-permute-start | bytes 786440 | tf_op jit(solution)/shard_map/ppermute | solution.py:12
  18.2 18.4 %collective-permute-start.2 = (bf16[256,512]{1,0:T(8,128)(2,1)}, bf16[256,512]{1,0:T(8,128)(2,1)}, u32[]{:S(2)}, u32[]{:S(2)}) collective-permute-start(bf16[256,512]{1,0:T(8,128)(2,1)} %param.7), channel_id=1, source_target_pairs={{0,32},{32,64},{64,96},{96,0},{1,33},{33,65},{65,97},{97,1},{2,34}... | collective-permute-start | bytes 786440 | tf_op jit(solution)/shard_map/ppermute | solution.py:12
  22.9 26.6 %collective-permute-start.7 = (bf16[1024,512]{0,1:T(8,128)(2,1)}, bf16[1024,512]{0,1:T(8,128)(2,1)}, u32[]{:S(2)}, u32[]{:S(2)}) collective-permute-start(bf16[1024,512]{0,1:T(8,128)(2,1)} %pad_maximum_fusion), channel_id=1, source_target_pairs={{0,128},{128,256},{256,384},{384,0},{1,129},{129,257},{257,385},{3... | collective-permute-start | bytes 3145736 | tf_op jit(solution)/shard_map/ppermute | solution.py:12
  26.0 27.7 %collective-permute-start.9 = (bf16[1024,512]{0,1:T(8,128)(2,1)}, bf16[1024,512]{0,1:T(8,128)(2,1)}, u32[]{:S(2)}, u32[]{:S(2)}) collective-permute-start(bf16[1024,512]{0,1:T(8,128)(2,1)} %pad_maximum_fusion.1), channel_id=1, source_target_pairs={{0,384},{128,0},{256,128},{384,256},{1,385},{129,1},{257,129},{385... | collective-permute-start | bytes 3145736 | tf_op jit(solution)/shard_map/ppermute | solution.py:12
  41.6 30.3 %collective-permute-start.4 = (bf16[1024,512]{1,0:T(8,128)(2,1)}, bf16[1024,512]{1,0:T(8,128)(2,1)}, u32[]{:S(2)}, u32[]{:S(2)}) collective-permute-start(bf16[1024,512]{1,0:T(8,128)(2,1)} %bitcast.8), channel_id=1, source_target_pairs={{0,128},{128,256},{256,384},{384,0},{1,129},{129,257},{257,385},{3... | collective-permute-start | bytes 3145736 | tf_op jit(solution)/shard_map/ppermute | solution.py:12
  45.0 31.2 %collective-permute-start.3 = (bf16[1024,512]{1,0:T(8,128)(2,1)}, bf16[1024,512]{1,0:T(8,128)(2,1)}, u32[]{:S(2)}, u32[]{:S(2)}) collective-permute-start(bf16[1024,512]{1,0:T(8,128)(2,1)} %bitcast.8), channel_id=1, source_target_pairs={{0,384},{128,0},{256,128},{384,256},{1,385},{129,1},{257,129},{385... | collective-permute-start | bytes 3145736 | tf_op jit(solution)/shard_map/ppermute | solution.py:12
  48.7 5.0 %copy-start.3 = (f32[1024,512]{0,1:T(8,128)S(1)}, f32[1024,512]{0,1:T(8,128)}, u32[]{:S(2)}) copy-start(f32[1024,512]{0,1:T(8,128)} %copy-done.2) | copy-start | bytes 6291460
  51.0 36.6 %collective-permute-start.8 = (bf16[512,512]{0,1:T(8,128)(2,1)S(1)}, bf16[512,512]{0,1:T(8,128)(2,1)S(1)}, u32[]{:S(2)}, u32[]{:S(2)}) collective-permute-start(bf16[512,512]{0,1:T(8,128)(2,1)S(1)} %add_convert_fusion.1), channel_id=1, source_target_pairs={{0,128},{128,256},{256,384},{384,0},{1,129},{129,257},{257,385},{3... | collective-permute-start | bytes 1572872 | tf_op jit(solution)/shard_map/ppermute | solution.py:12
  55.0 32.7 %collective-permute-start.10 = (bf16[512,512]{0,1:T(8,128)(2,1)S(1)}, bf16[512,512]{0,1:T(8,128)(2,1)S(1)}, u32[]{:S(2)}, u32[]{:S(2)}) collective-permute-start(bf16[512,512]{0,1:T(8,128)(2,1)S(1)} %add_convert_fusion), channel_id=1, source_target_pairs={{0,384},{128,0},{256,128},{384,256},{1,385},{129,1},{257,129},{385... | collective-permute-start | bytes 1572872 | tf_op jit(solution)/shard_map/ppermute | solution.py:12
  73.8 41.9 %collective-permute-start.5 = (bf16[512,512]{1,0:T(8,128)(2,1)}, bf16[512,512]{1,0:T(8,128)(2,1)}, u32[]{:S(2)}, u32[]{:S(2)}) collective-permute-start(bf16[512,512]{1,0:T(8,128)(2,1)} %slice.60), channel_id=1, source_target_pairs={{0,128},{128,256},{256,384},{384,0},{1,129},{129,257},{257,385},{3... | collective-permute-start | bytes 1572872 | tf_op jit(solution)/shard_map/ppermute | solution.py:12
  78.1 37.6 %collective-permute-start.6 = (bf16[512,512]{1,0:T(8,128)(2,1)}, bf16[512,512]{1,0:T(8,128)(2,1)}, u32[]{:S(2)}, u32[]{:S(2)}) collective-permute-start(bf16[512,512]{1,0:T(8,128)(2,1)} %slice.61), channel_id=1, source_target_pairs={{0,384},{128,0},{256,128},{384,256},{1,385},{129,1},{257,129},{385... | collective-permute-start | bytes 1572872 | tf_op jit(solution)/shard_map/ppermute | solution.py:12
  84.8 2.9 %copy-start.1 = (f32[1024,512]{0,1:T(8,128)S(1)}, f32[1024,512]{0,1:T(8,128)}, u32[]{:S(2)}) copy-start(f32[1024,512]{0,1:T(8,128)} %get-tuple-element.9) | copy-start | bytes 6291460
  89.8 20.7 %collective-permute-start.11 = (bf16[256,512]{0,1:T(8,128)(2,1)S(1)}, bf16[256,512]{0,1:T(8,128)(2,1)S(1)}, u32[]{:S(2)}, u32[]{:S(2)}) collective-permute-start(bf16[256,512]{0,1:T(8,128)(2,1)S(1)} %get-tuple-element.19), channel_id=1, source_target_pairs={{0,32},{32,64},{64,96},{96,0},{1,33},{33,65},{65,97},{97,1},{2,34}... | collective-permute-start | bytes 786440 | tf_op jit(solution)/shard_map/ppermute | solution.py:12
  93.1 20.2 %collective-permute-start.12 = (bf16[256,512]{0,1:T(8,128)(2,1)S(1)}, bf16[256,512]{0,1:T(8,128)(2,1)S(1)}, u32[]{:S(2)}, u32[]{:S(2)}) collective-permute-start(bf16[256,512]{0,1:T(8,128)(2,1)S(1)} %get-tuple-element.20), channel_id=1, source_target_pairs={{0,64},{32,96},{64,0},{96,32},{1,65},{33,97},{65,1},{97,33},{2,66}... | collective-permute-start | bytes 786440 | tf_op jit(solution)/shard_map/ppermute | solution.py:12
  97.1 17.5 %collective-permute-start.13 = (bf16[256,512]{0,1:T(8,128)(2,1)S(1)}, bf16[256,512]{0,1:T(8,128)(2,1)S(1)}, u32[]{:S(2)}, u32[]{:S(2)}) collective-permute-start(bf16[256,512]{0,1:T(8,128)(2,1)S(1)} %get-tuple-element.21), channel_id=1, source_target_pairs={{0,96},{32,0},{64,32},{96,64},{1,97},{33,1},{65,33},{97,65},{2,98}... | collective-permute-start | bytes 786440 | tf_op jit(solution)/shard_map/ppermute | solution.py:12

commit v4 on v3

--- a/solution.py
+++ b/solution.py
@@ -15,9 +15,7 @@
 def gather_line(x, axis, n):
     c = lax.axis_index(axis)
     parts = [x] + [_ring(x, axis, n, k) for k in range(1, n)]
-    stack = jnp.stack(parts[::-1] + parts[:0:-1])
-    out = lax.dynamic_slice_in_dim(stack, n - 1 - c, n, axis=0)
-    return out.reshape((n * x.shape[0],) + x.shape[1:])
+    return jnp.concatenate([lax.select_n((c - s) % n, *parts) for s in range(n)])
 
 
 def gather_ring4(x, axis):

time: 120 us -> 119 us (level)
  the two profiles are of different devices: /device:TPU:8 before, /device:TPU:184 now
where the time goes in v4:
time: 119 us; the launch traced here: 118 us
  starting transfers between devices  47.6 us (40%)
  waiting for transfers between devices  36.6 us (31%)
  matrix products  13.2 us (11%)
  local copies, waits for them, and re-layouts  9.8 us (8%)
  other arithmetic  9.67 us (8%)
    ppermute x14, starting transfers between devices, _ring(): return lax.ppermute(x, axis, [(i, (i + k) % n) for i in range(n)])  47.6 us
    ppermute x14, waiting for transfers between devices, _ring(): return lax.ppermute(x, axis, [(i, (i + k) % n) for i in range(n)])  36.6 us
    dot_general x4, matrix products, local(): term = jnp.dot(cols, blk, preferred_element_type=jnp.float32)  9.65 us
    dot_general x1, matrix products, local(): lax.dot_general(cotangent, hidden, (((0,), (0,)), ((), ())), preferred_el...  3.57 us
    unnamed x25, local copies, waits for them, and re-layouts  3.39 us
    dynamic_slice x2, local copies, waits for them, and re-layouts, local(): lax.dynamic_slice_in_dim(partial, (a + k) % ndp * span_rs, span_rs, axis=0)  2.46 us
  transfers between devices with their start and end apart: 14, of which 5 were waited for; matrix products, arithmetic and copies ran while one was open for 17% of the time, Pallas kernels for 0%

profile of v4, /device:TPU:184, one launch (start us, length us, event | category | flops | bytes accessed | tf_op | source)
XLA Modules:
  0.0 118.1 jit_solution(17514622645336259375)
XLA Ops:
  0.6 0.0 copy-start
  0.7 1.8 %copy-done = bf16[384,4096]{1,0:T(8,128)(2,1)S(1)} copy-done((bf16[384,4096]{1,0:T(8,128)(2,1)S(1)}, bf16[384,4096]{1,0:T(8,128)(2,1)}, u32[]{:S(2)}) %copy-start) | copy-done | bytes 3145752
  2.5 3.6 %fusion.30 = f32[512,4096]{1,0:T(8,128)S(1)} fusion(bf16[384,4096]{1,0:T(8,128)(2,1)S(1)} %copy-done, bf16[384,512]{1,0:T(8,128)(2,1)} %param.6, bf16[384,512]{1,0:T(8,128)(2,1)} %param.5), kind=kOutput, calls=%fused_computation.59 | convolution fusion | flops 1612185600 | bytes 12320768 | tf_op jit(solution)/shard_map/dot_general | solution.py:68
  6.1 0.2 dynamic-slice_bitcast_fusion.1
  6.3 0.0 copy-start.11
  6.3 2.3 %dynamic-slice_bitcast_fusion = (f32[1024,512]{0,1:T(8,128)S(1)}, f32[1024,512]{0,1:T(8,128)S(1)}, f32[1024,512]{0,1:T(8,128)}) fusion(f32[512,4096]{1,0:T(8,128)S(1)} %fusion.30, s32[]{:T(128)S(6)} %select_n.203, s32[]{:T(128)S(6)} %select_n.199, s32[]{:T(128)S(6)} %select_n.192), kind=kLoop, calls=%fused_computation.8 | loop fusion | bytes 12582924 | tf_op jit(solution)/shard_map/dynamic_slice | solution.py:71
  8.6 4.8 %collective-permute-start = (bf16[256,512]{1,0:T(8,128)(2,1)S(1)}, bf16[256,512]{1,0:T(8,128)(2,1)}, u32[]{:S(2)}, u32[]{:S(2)}) collective-permute-start(bf16[256,512]{1,0:T(8,128)(2,1)S(1)} %copy-done.11), channel_id=1, source_target_pairs={{0,32},{32,64},{64,96},{96,0},{1,33},{33,65},{65,97},{97,1},{2,34}... | collective-permute-start | bytes 786440 | tf_op jit(solution)/shard_map/ppermute | solution.py:12
  13.4 1.9 %collective-permute-start.1 = (bf16[256,512]{1,0:T(8,128)(2,1)S(1)}, bf16[256,512]{1,0:T(8,128)(2,1)}, u32[]{:S(2)}, u32[]{:S(2)}) collective-permute-start(bf16[256,512]{1,0:T(8,128)(2,1)S(1)} %copy-done.11), channel_id=1, source_target_pairs={{0,64},{32,96},{64,0},{96,32},{1,65},{33,97},{65,1},{97,33},{2,66}... | collective-permute-start | bytes 786440 | tf_op jit(solution)/shard_map/ppermute | solution.py:12
  15.3 3.1 %collective-permute-start.2 = (bf16[256,512]{1,0:T(8,128)(2,1)S(1)}, bf16[256,512]{1,0:T(8,128)(2,1)}, u32[]{:S(2)}, u32[]{:S(2)}) collective-permute-start(bf16[256,512]{1,0:T(8,128)(2,1)S(1)} %copy-done.11), channel_id=1, source_target_pairs={{0,96},{32,0},{64,32},{96,64},{1,97},{33,1},{65,33},{97,65},{2,98}... | collective-permute-start | bytes 786440 | tf_op jit(solution)/shard_map/ppermute | solution.py:12
  18.5 0.1 fusion.38
  18.6 0.1 slice.81
  18.6 1.1 pad_maximum_fusion.1
  19.8 3.4 %collective-permute-start.7 = (bf16[1024,512]{0,1:T(8,128)(2,1)}, bf16[1024,512]{0,1:T(8,128)(2,1)}, u32[]{:S(2)}, u32[]{:S(2)}) collective-permute-start(bf16[1024,512]{0,1:T(8,128)(2,1)} %pad_maximum_fusion.1), channel_id=1, source_target_pairs={{0,128},{128,256},{256,384},{384,0},{1,129},{129,257},{257,385},{3... | collective-permute-start | bytes 3145736 | tf_op jit(solution)/shard_map/ppermute | solution.py:12
  23.2 0.1 slice.80
  23.3 1.1 pad_maximum_fusion.2
  24.4 3.6 %collective-permute-start.9 = (bf16[1024,512]{0,1:T(8,128)(2,1)}, bf16[1024,512]{0,1:T(8,128)(2,1)}, u32[]{:S(2)}, u32[]{:S(2)}) collective-permute-start(bf16[1024,512]{0,1:T(8,128)(2,1)} %pad_maximum_fusion.2), channel_id=1, source_target_pairs={{0,384},{128,0},{256,128},{384,256},{1,385},{129,1},{257,129},{385... | collective-permute-start | bytes 3145736 | tf_op jit(solution)/shard_map/ppermute | solution.py:12
  28.1 8.2 %collective-permute-done.1 = bf16[256,512]{1,0:T(8,128)(2,1)} collective-permute-done((bf16[256,512]{1,0:T(8,128)(2,1)S(1)}, bf16[256,512]{1,0:T(8,128)(2,1)}, u32[]{:S(2)}, u32[]{:S(2)}) %collective-permute-start.1) | collective-permute-done | bytes 262176 | tf_op jit(solution)/shard_map/ppermute | solution.py:12
  36.3 1.3 %select_select_fusion.3 = (bf16[256,512]{1,0:T(8,128)(2,1)S(1)}, bf16[256,512]{1,0:T(8,128)(2,1)S(1)}, bf16[256,512]{1,0:T(8,128)(2,1)S(1)}, bf16[256,512]{1,0:T(8,128)(2,1)S(1)}) fusion(bf16[256,512]{1,0:T(8,128)(2,1)} %collective-permute-done.1, bf16[256,512]{1,0:T(8,128)(2,1)} %collective-permute-done.2, bf16[256,512]{1,0:T(8,128)(2,1)} %param.7, ...), kind=kLoop, calls=%fused_computation.63 | loop fusion | flops 1572864 | bytes 2097164 | tf_op jit(solution)/shard_map/select_n | solution.py:18
  37.6 0.0 copy-start.5
  37.6 0.0 copy-start.7
  37.6 0.0 copy-start.9
  37.6 0.7 copy-done.5
  38.3 1.1 pad_maximum_fusion
  39.3 3.4 %collective-permute-start.4 = (bf16[1024,512]{1,0:T(8,128)(2,1)}, bf16[1024,512]{1,0:T(8,128)(2,1)}, u32[]{:S(2)}, u32[]{:S(2)}) collective-permute-start(bf16[1024,512]{1,0:T(8,128)(2,1)} %pad_maximum_fusion), channel_id=1, source_target_pairs={{0,128},{128,256},{256,384},{384,0},{1,129},{129,257},{257,385},{3... | collective-permute-start | bytes 3145736 | tf_op jit(solution)/shard_map/ppermute | solution.py:12
  42.7 3.7 %collective-permute-start.3 = (bf16[1024,512]{1,0:T(8,128)(2,1)}, bf16[1024,512]{1,0:T(8,128)(2,1)}, u32[]{:S(2)}, u32[]{:S(2)}) collective-permute-start(bf16[1024,512]{1,0:T(8,128)(2,1)} %pad_maximum_fusion), channel_id=1, source_target_pairs={{0,384},{128,0},{256,128},{384,256},{1,385},{129,1},{257,129},{385... | collective-permute-start | bytes 3145736 | tf_op jit(solution)/shard_map/ppermute | solution.py:12
  46.5 2.8 %collective-permute-done.7 = bf16[1024,512]{0,1:T(8,128)(2,1)} collective-permute-done((bf16[1024,512]{0,1:T(8,128)(2,1)}, bf16[1024,512]{0,1:T(8,128)(2,1)}, u32[]{:S(2)}, u32[]{:S(2)}) %collective-permute-start.7) | collective-permute-done | bytes 1048608 | tf_op jit(solution)/shard_map/ppermute | solution.py:12
  49.3 1.5 %add_convert_fusion.1 = bf16[512,512]{0,1:T(8,128)(2,1)S(1)} fusion(f32[1024,512]{0,1:T(8,128)} %copy-done.4, bf16[1024,512]{0,1:T(8,128)(2,1)} %collective-permute-done.7), kind=kLoop, calls=%fused_computation.29 | loop fusion | flops 786432 | bytes 2097152 | tf_op jit(solution)/shard_map/convert_element_type | solution.py:38
  50.8 2.2 %collective-permute-start.8 = (bf16[512,512]{0,1:T(8,128)(2,1)S(1)}, bf16[512,512]{0,1:T(8,128)(2,1)S(1)}, u32[]{:S(2)}, u32[]{:S(2)}) collective-permute-start(bf16[512,512]{0,1:T(8,128)(2,1)S(1)} %add_convert_fusion.1), channel_id=1, source_target_pairs={{0,128},{128,256},{256,384},{384,0},{1,129},{129,257},{257,385},{3... | collective-permute-start | bytes 1572872 | tf_op jit(solution)/shard_map/ppermute | solution.py:12
  53.0 1.2 %add_convert_fusion = bf16[512,512]{0,1:T(8,128)(2,1)S(1)} fusion(f32[1024,512]{0,1:T(8,128)S(1)} %copy-done.3, bf16[1024,512]{0,1:T(8,128)(2,1)} %collective-permute-done.9), kind=kLoop, calls=%fused_computation.27 | loop fusion | flops 786432 | bytes 2097152 | tf_op jit(solution)/shard_map/convert_element_type | solution.py:39
  54.3 4.9 %collective-permute-start.10 = (bf16[512,512]{0,1:T(8,128)(2,1)S(1)}, bf16[512,512]{0,1:T(8,128)(2,1)S(1)}, u32[]{:S(2)}, u32[]{:S(2)}) collective-permute-start(bf16[512,512]{0,1:T(8,128)(2,1)S(1)} %add_convert_fusion), channel_id=1, source_target_pairs={{0,384},{128,0},{256,128},{384,256},{1,385},{129,1},{257,129},{385... | collective-permute-start | bytes 1572872 | tf_op jit(solution)/shard_map/ppermute | solution.py:12
  59.1 12.6 %collective-permute-done.4 = bf16[1024,512]{1,0:T(8,128)(2,1)} collective-permute-done((bf16[1024,512]{1,0:T(8,128)(2,1)}, bf16[1024,512]{1,0:T(8,128)(2,1)}, u32[]{:S(2)}, u32[]{:S(2)}) %collective-permute-start.4) | collective-permute-done | bytes 1048608 | tf_op jit(solution)/shard_map/ppermute | solution.py:12
  71.8 1.9 %slice.60 = bf16[512,512]{1,0:T(8,128)(2,1)} slice(bf16[1024,512]{1,0:T(8,128)(2,1)} %collective-permute-done.4), slice={[0:512], [0:512]} | slice | bytes 1048576 | tf_op jit(solution)/shard_map/slice | solution.py:25
  73.6 2.3 %collective-permute-start.5 = (bf16[512,512]{1,0:T(8,128)(2,1)}, bf16[512,512]{1,0:T(8,128)(2,1)}, u32[]{:S(2)}, u32[]{:S(2)}) collective-permute-start(bf16[512,512]{1,0:T(8,128)(2,1)} %slice.60), channel_id=1, source_target_pairs={{0,128},{128,256},{256,384},{384,0},{1,129},{129,257},{257,385},{3... | collective-permute-start | bytes 1572872 | tf_op jit(solution)/shard_map/ppermute | solution.py:12
  75.9 1.9 %slice.61 = bf16[512,512]{1,0:T(8,128)(2,1)} slice(bf16[1024,512]{1,0:T(8,128)(2,1)} %collective-permute-done.3), slice={[512:1024], [0:512]} | slice | bytes 1048576 | tf_op jit(solution)/shard_map/slice | solution.py:26
  77.8 4.9 %collective-permute-start.6 = (bf16[512,512]{1,0:T(8,128)(2,1)}, bf16[512,512]{1,0:T(8,128)(2,1)}, u32[]{:S(2)}, u32[]{:S(2)}) collective-permute-start(bf16[512,512]{1,0:T(8,128)(2,1)} %slice.61), channel_id=1, source_target_pairs={{0,384},{128,0},{256,128},{384,256},{1,385},{129,1},{257,129},{385... | collective-permute-start | bytes 1572872 | tf_op jit(solution)/shard_map/ppermute | solution.py:12
  82.7 1.8 %fusion.15 = f32[384,512]{1,0:T(8,128)S(1)} fusion(bf16[1024,512]{1,0:T(8,128)(2,1)} %collective-permute-done.3, bf16[384,4096]{1,0:T(8,128)(2,1)S(1)} %copy-done, s32[]{:T(128)S(6)} %select_n.199), kind=kOutput, calls=%fused_computation.44 | convolution fusion | flops 402653184 | bytes 2621444 | tf_op jit(solution)/shard_map/dot_general | solution.py:80
  84.5 1.5 %convolution_add_fusion.1 = f32[384,512]{1,0:T(8,128)} fusion(f32[384,512]{1,0:T(8,128)S(1)} %fusion.15, bf16[384,4096]{1,0:T(8,128)(2,1)S(1)} %copy-done, s32[]{:T(128)S(6)} %select_n.192, bf16[256,512]{1,0:T(8,128)(2,1)S(1)} %copy-done.6, bf16[256,512]{1,0:T(8,128)(2,1)S(1)} %copy-done.8, bf16[256,512]{1,0:T(8,128)(2,1)S(1)} %copy-done.10, ...), kind=kOutput, calls=%fused_computation.13 | convolution fusion | flops 407044096 | bytes 3407876 | tf_op jit(solution)/shard_map/dot_general | solution.py:80
  86.0 0.2 collective-permute-done.10
  86.3 1.7 %convert_add_fusion = (f32[512,512]{0,1:T(8,128)S(1)}, f32[512,512]{0,1:T(8,128)S(1)}) fusion(bf16[512,512]{0,1:T(8,128)(2,1)S(1)} %collective-permute-done.10, f32[1024,512]{0,1:T(8,128)S(1)} %copy-done.1, bf16[1024,512]{0,1:T(8,128)(2,1)} %collective-permute-done.7, bf16[1024,512]{0,1:T(8,128)(2,1)} %collective-permute-done.9, ...), kind=kLoop, calls=%fused_computation.26 | loop fusion | flops 2097152 | bytes 6291456 | tf_op jit(solution)/shard_map/add | solution.py:42
  87.9 0.4 fusion.27
  88.4 4.5 %collective-permute-start.11 = (bf16[256,512]{0,1:T(8,128)(2,1)S(1)}, bf16[256,512]{0,1:T(8,128)(2,1)S(1)}, u32[]{:S(2)}, u32[]{:S(2)}) collective-permute-start(bf16[256,512]{0,1:T(8,128)(2,1)S(1)} %get-tuple-element.19), channel_id=1, source_target_pairs={{0,32},{32,64},{64,96},{96,0},{1,33},{33,65},{65,97},{97,1},{2,34}... | collective-permute-start | bytes 786440 | tf_op jit(solution)/shard_map/ppermute | solution.py:12
  92.9 3.0 %collective-permute-start.12 = (bf16[256,512]{0,1:T(8,128)(2,1)S(1)}, bf16[256,512]{0,1:T(8,128)(2,1)S(1)}, u32[]{:S(2)}, u32[]{:S(2)}) collective-permute-start(bf16[256,512]{0,1:T(8,128)(2,1)S(1)} %get-tuple-element.20), channel_id=1, source_target_pairs={{0,64},{32,96},{64,0},{96,32},{1,65},{33,97},{65,1},{97,33},{2,66}... | collective-permute-start | bytes 786440 | tf_op jit(solution)/shard_map/ppermute | solution.py:12
  95.9 1.9 %collective-permute-start.13 = (bf16[256,512]{0,1:T(8,128)(2,1)S(1)}, bf16[256,512]{0,1:T(8,128)(2,1)S(1)}, u32[]{:S(2)}, u32[]{:S(2)}) collective-permute-start(bf16[256,512]{0,1:T(8,128)(2,1)S(1)} %get-tuple-element.21), channel_id=1, source_target_pairs={{0,96},{32,0},{64,32},{96,64},{1,97},{33,1},{65,33},{97,65},{2,98}... | collective-permute-start | bytes 786440 | tf_op jit(solution)/shard_map/ppermute | solution.py:12
  97.8 2.7 %fusion.12 = f32[384,512]{1,0:T(8,128)} fusion(bf16[1024,512]{1,0:T(8,128)(2,1)} %collective-permute-done.4, bf16[384,4096]{1,0:T(8,128)(2,1)S(1)} %copy-done, s32[]{:T(128)S(6)} %select_n.203), kind=kOutput, calls=%fused_computation.41 | convolution fusion | flops 402653184 | bytes 2621444 | tf_op jit(solution)/shard_map/dot_general | solution.py:80
  100.6 12.8 %collective-permute-done.12 = bf16[256,512]{0,1:T(8,128)(2,1)S(1)} collective-permute-done((bf16[256,512]{0,1:T(8,128)(2,1)S(1)}, bf16[256,512]{0,1:T(8,128)(2,1)S(1)}, u32[]{:S(2)}, u32[]{:S(2)}) %collective-permute-start.12) | collective-permute-done | bytes 262176 | tf_op jit(solution)/shard_map/ppermute | solution.py:12
  113.4 0.2 fusion.25
  113.6 0.8 copy.7
  114.4 3.7 %multiply_convert_fusion = (bf16[384,512]{1,0:T(8,128)(2,1)}, bf16[384,512]{1,0:T(8,128)(2,1)}) fusion(bf16[384,512]{1,0:T(8,128)(2,1)} %param.5, bf16[384,512]{1,0:T(8,128)(2,1)} %param.6, f32[384,512]{1,0:T(8,128)} %fusion.12, f32[384,512]{1,0:T(8,128)} %convolution_add_fusion.1, bf16[512,512]{1,0:T(8,128)(2,1)} %collective-permute-done.6, ...), kind=kOutput, calls=%fused_computation.40 | convolution fusion | flops 408092672 | bytes 4980740 | tf_op jit(solution)/shard_map/dot_general | solution.py:80
  (26 shorter events, 0.1 us)
Async XLA Ops:
  0.6 1.9 %copy-start = (bf16[384,4096]{1,0:T(8,128)(2,1)S(1)}, bf16[384,4096]{1,0:T(8,128)(2,1)}, u32[]{:S(2)}) copy-start(bf16[384,4096]{1,0:T(8,128)(2,1)} %param.4) | copy-start | bytes 9437188
  6.3 2.3 %copy-start.11 = (bf16[256,512]{1,0:T(8,128)(2,1)S(1)}, bf16[256,512]{1,0:T(8,128)(2,1)}, u32[]{:S(2)}) copy-start(bf16[256,512]{1,0:T(8,128)(2,1)} %param.7) | copy-start | bytes 786436
  8.6 11.2 %copy-start.4 = (f32[1024,512]{0,1:T(8,128)}, f32[1024,512]{0,1:T(8,128)S(1)}, u32[]{:S(2)}) copy-start(f32[1024,512]{0,1:T(8,128)S(1)} %get-tuple-element.10) | copy-start | bytes 6291460
  8.6 14.6 %copy-start.2 = (f32[1024,512]{0,1:T(8,128)}, f32[1024,512]{0,1:T(8,128)S(1)}, u32[]{:S(2)}) copy-start(f32[1024,512]{0,1:T(8,128)S(1)} %get-tuple-element.12) | copy-start | bytes 6291460
  8.6 19.5 %collective-permute-start = (bf16[256,512]{1,0:T(8,128)(2,1)S(1)}, bf16[256,512]{1,0:T(8,128)(2,1)}, u32[]{:S(2)}, u32[]{:S(2)}) collective-permute-start(bf16[256,512]{1,0:T(8,128)(2,1)S(1)} %copy-done.11), channel_id=1, source_target_pairs={{0,32},{32,64},{64,96},{96,0},{1,33},{33,65},{65,97},{97,1},{2,34}... | collective-permute-start | bytes 786440 | tf_op jit(solution)/shard_map/ppermute | solution.py:12
  13.4 22.8 %collective-permute-start.1 = (bf16[256,512]{1,0:T(8,128)(2,1)S(1)}, bf16[256,512]{1,0:T(8,128)(2,1)}, u32[]{:S(2)}, u32[]{:S(2)}) collective-permute-start(bf16[256,512]{1,0:T(8,128)(2,1)S(1)} %copy-done.11), channel_id=1, source_target_pairs={{0,64},{32,96},{64,0},{96,32},{1,65},{33,97},{65,1},{97,33},{2,66}... | collective-permute-start | bytes 786440 | tf_op jit(solution)/shard_map/ppermute | solution.py:12
  15.3 20.9 %collective-permute-start.2 = (bf16[256,512]{1,0:T(8,128)(2,1)S(1)}, bf16[256,512]{1,0:T(8,128)(2,1)}, u32[]{:S(2)}, u32[]{:S(2)}) collective-permute-start(bf16[256,512]{1,0:T(8,128)(2,1)S(1)} %copy-done.11), channel_id=1, source_target_pairs={{0,96},{32,0},{64,32},{96,64},{1,97},{33,1},{65,33},{97,65},{2,98}... | collective-permute-start | bytes 786440 | tf_op jit(solution)/shard_map/ppermute | solution.py:12
  19.8 29.5 %collective-permute-start.7 = (bf16[1024,512]{0,1:T(8,128)(2,1)}, bf16[1024,512]{0,1:T(8,128)(2,1)}, u32[]{:S(2)}, u32[]{:S(2)}) collective-permute-start(bf16[1024,512]{0,1:T(8,128)(2,1)} %pad_maximum_fusion.1), channel_id=1, source_target_pairs={{0,128},{128,256},{256,384},{384,0},{1,129},{129,257},{257,385},{3... | collective-permute-start | bytes 3145736 | tf_op jit(solution)/shard_map/ppermute | solution.py:12
  24.4 28.6 %collective-permute-start.9 = (bf16[1024,512]{0,1:T(8,128)(2,1)}, bf16[1024,512]{0,1:T(8,128)(2,1)}, u32[]{:S(2)}, u32[]{:S(2)}) collective-permute-start(bf16[1024,512]{0,1:T(8,128)(2,1)} %pad_maximum_fusion.2), channel_id=1, source_target_pairs={{0,384},{128,0},{256,128},{384,256},{1,385},{129,1},{257,129},{385... | collective-permute-start | bytes 3145736 | tf_op jit(solution)/shard_map/ppermute | solution.py:12
  37.6 0.7 copy-start.5
  37.6 1.8 %copy-start.7 = (bf16[256,512]{1,0:T(8,128)(2,1)}, bf16[256,512]{1,0:T(8,128)(2,1)S(1)}, u32[]{:S(2)}) copy-start(bf16[256,512]{1,0:T(8,128)(2,1)S(1)} %get-tuple-element.30) | copy-start | bytes 786436
  37.6 5.1 %copy-start.9 = (bf16[256,512]{1,0:T(8,128)(2,1)}, bf16[256,512]{1,0:T(8,128)(2,1)S(1)}, u32[]{:S(2)}) copy-start(bf16[256,512]{1,0:T(8,128)(2,1)S(1)} %get-tuple-element.31) | copy-start | bytes 786436
  39.3 32.4 %collective-permute-start.4 = (bf16[1024,512]{1,0:T(8,128)(2,1)}, bf16[1024,512]{1,0:T(8,128)(2,1)}, u32[]{:S(2)}, u32[]{:S(2)}) collective-permute-start(bf16[1024,512]{1,0:T(8,128)(2,1)} %pad_maximum_fusion), channel_id=1, source_target_pairs={{0,128},{128,256},{256,384},{384,0},{1,129},{129,257},{257,385},{3... | collective-permute-start | bytes 3145736 | tf_op jit(solution)/shard_map/ppermute | solution.py:12
  42.7 33.2 %collective-permute-start.3 = (bf16[1024,512]{1,0:T(8,128)(2,1)}, bf16[1024,512]{1,0:T(8,128)(2,1)}, u32[]{:S(2)}, u32[]{:S(2)}) collective-permute-start(bf16[1024,512]{1,0:T(8,128)(2,1)} %pad_maximum_fusion), channel_id=1, source_target_pairs={{0,384},{128,0},{256,128},{384,256},{1,385},{129,1},{257,129},{385... | collective-permute-start | bytes 3145736 | tf_op jit(solution)/shard_map/ppermute | solution.py:12
  46.5 6.6 %copy-start.3 = (f32[1024,512]{0,1:T(8,128)S(1)}, f32[1024,512]{0,1:T(8,128)}, u32[]{:S(2)}) copy-start(f32[1024,512]{0,1:T(8,128)} %copy-done.2) | copy-start | bytes 6291460
  50.8 35.2 %collective-permute-start.8 = (bf16[512,512]{0,1:T(8,128)(2,1)S(1)}, bf16[512,512]{0,1:T(8,128)(2,1)S(1)}, u32[]{:S(2)}, u32[]{:S(2)}) collective-permute-start(bf16[512,512]{0,1:T(8,128)(2,1)S(1)} %add_convert_fusion.1), channel_id=1, source_target_pairs={{0,128},{128,256},{256,384},{384,0},{1,129},{129,257},{257,385},{3... | collective-permute-start | bytes 1572872 | tf_op jit(solution)/shard_map/ppermute | solution.py:12
  54.3 32.0 %collective-permute-start.10 = (bf16[512,512]{0,1:T(8,128)(2,1)S(1)}, bf16[512,512]{0,1:T(8,128)(2,1)S(1)}, u32[]{:S(2)}, u32[]{:S(2)}) collective-permute-start(bf16[512,512]{0,1:T(8,128)(2,1)S(1)} %add_convert_fusion), channel_id=1, source_target_pairs={{0,384},{128,0},{256,128},{384,256},{1,385},{129,1},{257,129},{385... | collective-permute-start | bytes 1572872 | tf_op jit(solution)/shard_map/ppermute | solution.py:12
  73.6 10.9 %copy-start.6 = (bf16[256,512]{1,0:T(8,128)(2,1)S(1)}, bf16[256,512]{1,0:T(8,128)(2,1)}, u32[]{:S(2)}) copy-start(bf16[256,512]{1,0:T(8,128)(2,1)} %copy-done.5) | copy-start | bytes 786436
  73.6 10.9 %copy-start.8 = (bf16[256,512]{1,0:T(8,128)(2,1)S(1)}, bf16[256,512]{1,0:T(8,128)(2,1)}, u32[]{:S(2)}) copy-start(bf16[256,512]{1,0:T(8,128)(2,1)} %copy-done.7) | copy-start | bytes 786436
  73.6 10.9 %copy-start.10 = (bf16[256,512]{1,0:T(8,128)(2,1)S(1)}, bf16[256,512]{1,0:T(8,128)(2,1)}, u32[]{:S(2)}) copy-start(bf16[256,512]{1,0:T(8,128)(2,1)} %copy-done.9) | copy-start | bytes 786436
  73.6 40.8 %collective-permute-start.5 = (bf16[512,512]{1,0:T(8,128)(2,1)}, bf16[512,512]{1,0:T(8,128)(2,1)}, u32[]{:S(2)}, u32[]{:S(2)}) collective-permute-start(bf16[512,512]{1,0:T(8,128)(2,1)} %slice.60), channel_id=1, source_target_pairs={{0,128},{128,256},{256,384},{384,0},{1,129},{129,257},{257,385},{3... | collective-permute-start | bytes 1572872 | tf_op jit(solution)/shard_map/ppermute | solution.py:12
  77.8 36.6 %collective-permute-start.6 = (bf16[512,512]{1,0:T(8,128)(2,1)}, bf16[512,512]{1,0:T(8,128)(2,1)}, u32[]{:S(2)}, u32[]{:S(2)}) collective-permute-start(bf16[512,512]{1,0:T(8,128)(2,1)} %slice.61), channel_id=1, source_target_pairs={{0,384},{128,0},{256,128},{384,256},{1,385},{129,1},{257,129},{385... | collective-permute-start | bytes 1572872 | tf_op jit(solution)/shard_map/ppermute | solution.py:12
  84.5 1.7 %copy-start.1 = (f32[1024,512]{0,1:T(8,128)S(1)}, f32[1024,512]{0,1:T(8,128)}, u32[]{:S(2)}) copy-start(f32[1024,512]{0,1:T(8,128)} %get-tuple-element.9) | copy-start | bytes 6291460
  88.4 12.2 %collective-permute-start.11 = (bf16[256,512]{0,1:T(8,128)(2,1)S(1)}, bf16[256,512]{0,1:T(8,128)(2,1)S(1)}, u32[]{:S(2)}, u32[]{:S(2)}) collective-permute-start(bf16[256,512]{0,1:T(8,128)(2,1)S(1)} %get-tuple-element.19), channel_id=1, source_target_pairs={{0,32},{32,64},{64,96},{96,0},{1,33},{33,65},{65,97},{97,1},{2,34}... | collective-permute-start | bytes 786440 | tf_op jit(solution)/shard_map/ppermute | solution.py:12
  92.9 20.5 %collective-permute-start.12 = (bf16[256,512]{0,1:T(8,128)(2,1)S(1)}, bf16[256,512]{0,1:T(8,128)(2,1)S(1)}, u32[]{:S(2)}, u32[]{:S(2)}) collective-permute-start(bf16[256,512]{0,1:T(8,128)(2,1)S(1)} %get-tuple-element.20), channel_id=1, source_target_pairs={{0,64},{32,96},{64,0},{96,32},{1,65},{33,97},{65,1},{97,33},{2,66}... | collective-permute-start | bytes 786440 | tf_op jit(solution)/shard_map/ppermute | solution.py:12
  95.9 17.4 %collective-permute-start.13 = (bf16[256,512]{0,1:T(8,128)(2,1)S(1)}, bf16[256,512]{0,1:T(8,128)(2,1)S(1)}, u32[]{:S(2)}, u32[]{:S(2)}) collective-permute-start(bf16[256,512]{0,1:T(8,128)(2,1)S(1)} %get-tuple-element.21), channel_id=1, source_target_pairs={{0,96},{32,0},{64,32},{96,64},{1,97},{33,1},{65,33},{97,65},{2,98}... | collective-permute-start | bytes 786440 | tf_op jit(solution)/shard_map/ppermute | solution.py:12

commit v5 on v4

--- a/solution.py
+++ b/solution.py
@@ -71,7 +71,8 @@
     blocks = [lax.dynamic_slice_in_dim(partial, ((a + k) % ndp) * span_rs, span_rs, axis=0) for k in range(4)]
     w_down, blocks = lax.optimization_barrier((w_down, blocks))
     reduced = scatter_ring4(blocks, "dp")
-    summed = scatter_line(reduced, "ctx", nctx)
+    got = lax.all_to_all(reduced.astype(jnp.bfloat16), "ctx", 0, 0, tiled=True)
+    summed = got.astype(jnp.float32).reshape((nctx, -1) + got.shape[1:]).sum(axis=0)
     w_ctx = gather_line(w_down, "ctx", nctx)
     span = w_ctx.shape[0]
     grad_hidden = None

time: 119 us -> 109 us (0.916)
  the two profiles are of different devices: /device:TPU:184 before, /device:TPU:454 now
where the time goes in v5:
time: 109 us; the launch traced here: 108 us
  starting transfers between devices  43.9 us (40%)
  waiting for transfers between devices  33.4 us (31%)
  other arithmetic  10.9 us (10%)
  matrix products  9.52 us (9%)
  local copies, waits for them, and re-layouts  8.8 us (8%)
  between operations  1.18 us (1%)
    ppermute x11, starting transfers between devices, _ring(): return lax.ppermute(x, axis, [(i, (i + k) % n) for i in range(n)])  39.1 us
    ppermute x11, waiting for transfers between devices, _ring(): return lax.ppermute(x, axis, [(i, (i + k) % n) for i in range(n)])  33.4 us
    dot_general x4, matrix products, local(): term = jnp.dot(cols, blk, preferred_element_type=jnp.float32)  5.95 us
    all_to_all x1, starting transfers between devices, local(): got = lax.all_to_all(reduced.astype(jnp.bfloat16), 'ctx', 0, 0, tiled=True)  4.87 us
    dot_general x1, matrix products, local(): lax.dot_general(cotangent, hidden, (((0,), (0,)), ((), ())), preferred_el...  3.57 us
    unnamed x31, local copies, waits for them, and re-layouts  2.93 us
    dynamic_slice x2, local copies, waits for them, and re-layouts, local(): lax.dynamic_slice_in_dim(partial, (a + k) % ndp * span_rs, span_rs, axis=0)  2.46 us
  transfers between devices with their start and end apart: 12, of which 5 were waited for; matrix products, arithmetic and copies ran while one was open for 16% of the time, Pallas kernels for 0%

profile of v5, /device:TPU:454, one launch (start us, length us, event | category | flops | bytes accessed | tf_op | source)
XLA Modules:
  0.0 107.8 jit_solution(462255086421328187)
XLA Ops:
  0.6 0.0 copy-start
  0.7 1.8 %copy-done = bf16[384,4096]{1,0:T(8,128)(2,1)S(1)} copy-done((bf16[384,4096]{1,0:T(8,128)(2,1)S(1)}, bf16[384,4096]{1,0:T(8,128)(2,1)}, u32[]{:S(2)}) %copy-start) | copy-done | bytes 3145752
  2.5 3.6 %fusion.18 = f32[512,4096]{1,0:T(8,128)S(1)} fusion(bf16[384,4096]{1,0:T(8,128)(2,1)S(1)} %copy-done, bf16[384,512]{1,0:T(8,128)(2,1)} %param.6, bf16[384,512]{1,0:T(8,128)(2,1)} %param.5), kind=kOutput, calls=%fused_computation.43 | convolution fusion | flops 1612185600 | bytes 12320768 | tf_op jit(solution)/shard_map/dot_general | solution.py:68
  6.1 0.2 dynamic-slice_bitcast_fusion.1
  6.3 2.3 %dynamic-slice_bitcast_fusion = (f32[1024,512]{0,1:T(8,128)S(1)}, f32[1024,512]{0,1:T(8,128)S(1)}, f32[1024,512]{0,1:T(8,128)}) fusion(f32[512,4096]{1,0:T(8,128)S(1)} %fusion.18, s32[]{:T(128)S(6)} %select_n.179, s32[]{:T(128)S(6)} %select_n.175, s32[]{:T(128)S(6)} %select_n.168), kind=kLoop, calls=%fused_computation.1 | loop fusion | bytes 12582924 | tf_op jit(solution)/shard_map/dynamic_slice | solution.py:71
  8.6 0.1 fusion.26
  8.6 0.1 slice.80
  8.7 1.4 %pad_maximum_fusion.2 = bf16[1024,512]{0,1:T(8,128)(2,1)} fusion(bf16[512,512]{0,1:T(8,128)(2,1)S(1)} %get-tuple-element.24, bf16[512,512]{0,1:T(8,128)(2,1)S(1)} %slice.80), kind=kLoop, calls=%fused_computation.19 | loop fusion | flops 2097152 | bytes 2097152 | tf_op jit(solution)/shard_map/concatenate | solution.py:35
  10.1 0.2 copy-done.4
  10.3 2.9 %collective-permute-start.9 = (bf16[1024,512]{0,1:T(8,128)(2,1)}, bf16[1024,512]{0,1:T(8,128)(2,1)}, u32[]{:S(2)}, u32[]{:S(2)}) collective-permute-start(bf16[1024,512]{0,1:T(8,128)(2,1)} %pad_maximum_fusion.2), channel_id=1, source_target_pairs={{0,384},{128,0},{256,128},{384,256},{1,385},{129,1},{257,129},{385... | collective-permute-start | bytes 3145736 | tf_op jit(solution)/shard_map/ppermute | solution.py:12
  13.2 0.1 slice.81
  13.3 1.2 %pad_maximum_fusion.1 = bf16[1024,512]{0,1:T(8,128)(2,1)} fusion(bf16[512,512]{0,1:T(8,128)(2,1)S(1)} %get-tuple-element.23, bf16[512,512]{0,1:T(8,128)(2,1)S(1)} %slice.81), kind=kLoop, calls=%fused_computation.18 | loop fusion | flops 2097152 | bytes 2097152 | tf_op jit(solution)/shard_map/concatenate | solution.py:34
  14.5 4.3 %collective-permute-start.7 = (bf16[1024,512]{0,1:T(8,128)(2,1)}, bf16[1024,512]{0,1:T(8,128)(2,1)}, u32[]{:S(2)}, u32[]{:S(2)}) collective-permute-start(bf16[1024,512]{0,1:T(8,128)(2,1)} %pad_maximum_fusion.1), channel_id=1, source_target_pairs={{0,128},{128,256},{256,384},{384,0},{1,129},{129,257},{257,385},{3... | collective-permute-start | bytes 3145736 | tf_op jit(solution)/shard_map/ppermute | solution.py:12
  18.8 3.5 %collective-permute-start = (bf16[256,512]{1,0:T(8,128)(2,1)S(1)}, bf16[256,512]{1,0:T(8,128)(2,1)}, u32[]{:S(2)}, u32[]{:S(2)}) collective-permute-start(bf16[256,512]{1,0:T(8,128)(2,1)S(1)} %copy-done.13), channel_id=1, source_target_pairs={{0,32},{32,64},{64,96},{96,0},{1,33},{33,65},{65,97},{97,1},{2,34}... | collective-permute-start | bytes 786440 | tf_op jit(solution)/shard_map/ppermute | solution.py:12
  22.3 4.5 %collective-permute-start.1 = (bf16[256,512]{1,0:T(8,128)(2,1)S(1)}, bf16[256,512]{1,0:T(8,128)(2,1)}, u32[]{:S(2)}, u32[]{:S(2)}) collective-permute-start(bf16[256,512]{1,0:T(8,128)(2,1)S(1)} %copy-done.13), channel_id=1, source_target_pairs={{0,64},{32,96},{64,0},{96,32},{1,65},{33,97},{65,1},{97,33},{2,66}... | collective-permute-start | bytes 786440 | tf_op jit(solution)/shard_map/ppermute | solution.py:12
  26.8 3.3 %collective-permute-start.2 = (bf16[256,512]{1,0:T(8,128)(2,1)S(1)}, bf16[256,512]{1,0:T(8,128)(2,1)}, u32[]{:S(2)}, u32[]{:S(2)}) collective-permute-start(bf16[256,512]{1,0:T(8,128)(2,1)S(1)} %copy-done.13), channel_id=1, source_target_pairs={{0,96},{32,0},{64,32},{96,64},{1,97},{33,1},{65,33},{97,65},{2,98}... | collective-permute-start | bytes 786440 | tf_op jit(solution)/shard_map/ppermute | solution.py:12
  30.1 0.0 copy-start.14
  30.2 8.6 %collective-permute-done.9 = bf16[1024,512]{0,1:T(8,128)(2,1)} collective-permute-done((bf16[1024,512]{0,1:T(8,128)(2,1)}, bf16[1024,512]{0,1:T(8,128)(2,1)}, u32[]{:S(2)}, u32[]{:S(2)}) %collective-permute-start.9) | collective-permute-done | bytes 1048608 | tf_op jit(solution)/shard_map/ppermute | solution.py:12
  38.8 1.5 %add_convert_fusion.1 = bf16[512,512]{0,1:T(8,128)(2,1)S(1)} fusion(f32[1024,512]{0,1:T(8,128)} %copy-done.4, bf16[1024,512]{0,1:T(8,128)(2,1)} %collective-permute-done.9), kind=kLoop, calls=%fused_computation.22 | loop fusion | flops 786432 | bytes 2097152 | tf_op jit(solution)/shard_map/convert_element_type | solution.py:39
  40.3 1.9 %collective-permute-start.10 = (bf16[512,512]{0,1:T(8,128)(2,1)S(1)}, bf16[512,512]{0,1:T(8,128)(2,1)S(1)}, u32[]{:S(2)}, u32[]{:S(2)}) collective-permute-start(bf16[512,512]{0,1:T(8,128)(2,1)S(1)} %add_convert_fusion.1), channel_id=1, source_target_pairs={{0,384},{128,0},{256,128},{384,256},{1,385},{129,1},{257,129},{385... | collective-permute-start | bytes 1572872 | tf_op jit(solution)/shard_map/ppermute | solution.py:12
  42.2 1.2 %add_convert_fusion.3 = bf16[512,512]{0,1:T(8,128)(2,1)S(1)} fusion(f32[1024,512]{0,1:T(8,128)S(1)} %copy-done.3, bf16[1024,512]{0,1:T(8,128)(2,1)} %collective-permute-done.7), kind=kLoop, calls=%fused_computation.24 | loop fusion | flops 786432 | bytes 2097152 | tf_op jit(solution)/shard_map/convert_element_type | solution.py:38
  43.5 5.3 %collective-permute-start.8 = (bf16[512,512]{0,1:T(8,128)(2,1)S(1)}, bf16[512,512]{0,1:T(8,128)(2,1)S(1)}, u32[]{:S(2)}, u32[]{:S(2)}) collective-permute-start(bf16[512,512]{0,1:T(8,128)(2,1)S(1)} %add_convert_fusion.3), channel_id=1, source_target_pairs={{0,128},{128,256},{256,384},{384,0},{1,129},{129,257},{257,385},{3... | collective-permute-start | bytes 1572872 | tf_op jit(solution)/shard_map/ppermute | solution.py:12
  48.8 1.2 %select_select_fusion.3 = (bf16[256,512]{1,0:T(8,128)(2,1)S(1)}, bf16[256,512]{1,0:T(8,128)(2,1)S(1)}, bf16[256,512]{1,0:T(8,128)(2,1)S(1)}, bf16[256,512]{1,0:T(8,128)(2,1)S(1)}) fusion(bf16[256,512]{1,0:T(8,128)(2,1)} %collective-permute-done.1, bf16[256,512]{1,0:T(8,128)(2,1)} %collective-permute-done.2, bf16[256,512]{1,0:T(8,128)(2,1)S(1)} %copy-done.14, ...), kind=kLoop, calls=%fused_computation.47 | loop fusion | flops 1572864 | bytes 2097164 | tf_op jit(solution)/shard_map/select_n | solution.py:18
  50.0 0.0 copy-start.5
  50.0 0.0 copy-start.7
  50.0 1.1 %pad_maximum_fusion = bf16[1024,512]{1,0:T(8,128)(2,1)} fusion(bf16[256,512]{1,0:T(8,128)(2,1)S(1)} %get-tuple-element.26, bf16[256,512]{1,0:T(8,128)(2,1)S(1)} %get-tuple-element.27, bf16[256,512]{1,0:T(8,128)(2,1)S(1)} %get-tuple-element.28, bf16[256,512]{1,0:T(8,128)(2,1)S(1)} %get-tuple-element.25), kind=kLoop, calls=%fused_computation.14 | loop fusion | flops 4194304 | bytes 2097152 | tf_op jit(solution)/shard_map/concatenate | solution.py:18
  51.2 1.9 %collective-permute-start.4 = (bf16[1024,512]{1,0:T(8,128)(2,1)}, bf16[1024,512]{1,0:T(8,128)(2,1)}, u32[]{:S(2)}, u32[]{:S(2)}) collective-permute-start(bf16[1024,512]{1,0:T(8,128)(2,1)} %pad_maximum_fusion), channel_id=1, source_target_pairs={{0,128},{128,256},{256,384},{384,0},{1,129},{129,257},{257,385},{3... | collective-permute-start | bytes 3145736 | tf_op jit(solution)/shard_map/ppermute | solution.py:12
  53.1 3.9 %collective-permute-start.3 = (bf16[1024,512]{1,0:T(8,128)(2,1)}, bf16[1024,512]{1,0:T(8,128)(2,1)}, u32[]{:S(2)}, u32[]{:S(2)}) collective-permute-start(bf16[1024,512]{1,0:T(8,128)(2,1)} %pad_maximum_fusion), channel_id=1, source_target_pairs={{0,384},{128,0},{256,128},{384,256},{1,385},{129,1},{257,129},{385... | collective-permute-start | bytes 3145736 | tf_op jit(solution)/shard_map/ppermute | solution.py:12
  57.1 4.0 %collective-permute-done.8 = bf16[512,512]{0,1:T(8,128)(2,1)S(1)} collective-permute-done((bf16[512,512]{0,1:T(8,128)(2,1)S(1)}, bf16[512,512]{0,1:T(8,128)(2,1)S(1)}, u32[]{:S(2)}, u32[]{:S(2)}) %collective-permute-start.8) | collective-permute-done | bytes 524320 | tf_op jit(solution)/shard_map/ppermute | solution.py:12
  61.1 1.7 %add_convert_fusion.2 = (bf16[512,512]{0,1:T(8,128)(2,1)S(1)}, bf16[512,512]{0,1:T(8,128)(2,1)S(1)}) fusion(bf16[512,512]{0,1:T(8,128)(2,1)S(1)} %collective-permute-done.8, f32[1024,512]{0,1:T(8,128)S(1)} %copy-done.1, bf16[1024,512]{0,1:T(8,128)(2,1)} %collective-permute-done.9, bf16[512,512]{0,1:T(8,128)(2,1)S(1)} %collective-permute-done.10, ...), kind=kLoop, calls=%fused_computation.23 | loop fusion | flops 2621440 | bytes 5242880 | tf_op jit(solution)/shard_map/convert
  62.8 0.1 pad_maximum_fusion.3
  62.9 1.0 copy.13
  63.9 4.9 %all-to-all-start = ((bf16[4,256,512]{1,2,0:T(8,128)(2,1)}), bf16[4,256,512]{1,2,0:T(8,128)(2,1)}, u32[]{:S(2)}, u32[]{:S(2)}) async-start(bf16[4,256,512]{1,2,0:T(8,128)(2,1)} %bitcast.15), calls=%async_computation | async-start | bytes 2097152 | tf_op jit(solution)/shard_map/all_to_all | solution.py:74
  68.8 12.5 %collective-permute-done.4 = bf16[1024,512]{1,0:T(8,128)(2,1)} collective-permute-done((bf16[1024,512]{1,0:T(8,128)(2,1)}, bf16[1024,512]{1,0:T(8,128)(2,1)}, u32[]{:S(2)}, u32[]{:S(2)}) %collective-permute-start.4) | collective-permute-done | bytes 1048608 | tf_op jit(solution)/shard_map/ppermute | solution.py:12
  81.3 1.1 slice.60
  82.4 5.6 %collective-permute-start.5 = (bf16[512,512]{1,0:T(8,128)(2,1)S(1)}, bf16[512,512]{1,0:T(8,128)(2,1)S(1)}, u32[]{:S(2)}, u32[]{:S(2)}) collective-permute-start(bf16[512,512]{1,0:T(8,128)(2,1)S(1)} %slice.60), channel_id=1, source_target_pairs={{0,128},{128,256},{256,384},{384,0},{1,129},{129,257},{257,385},{3... | collective-permute-start | bytes 1572872 | tf_op jit(solution)/shard_map/ppermute | solution.py:12
  88.0 1.1 slice.61
  89.1 0.0 copy-start.8
  89.1 0.0 copy-start.10
  89.1 2.1 %collective-permute-start.6 = (bf16[512,512]{1,0:T(8,128)(2,1)S(1)}, bf16[512,512]{1,0:T(8,128)(2,1)S(1)}, u32[]{:S(2)}, u32[]{:S(2)}) collective-permute-start(bf16[512,512]{1,0:T(8,128)(2,1)S(1)} %slice.61), channel_id=1, source_target_pairs={{0,384},{128,0},{256,128},{384,256},{1,385},{129,1},{257,129},{385... | collective-permute-start | bytes 1572872 | tf_op jit(solution)/shard_map/ppermute | solution.py:12
  91.2 1.8 %fusion.15 = f32[384,512]{1,0:T(8,128)S(1)} fusion(bf16[1024,512]{1,0:T(8,128)(2,1)} %collective-permute-done.3, bf16[384,4096]{1,0:T(8,128)(2,1)S(1)} %copy-done, s32[]{:T(128)S(6)} %select_n.175), kind=kOutput, calls=%fused_computation.39 | convolution fusion | flops 402653184 | bytes 2621444 | tf_op jit(solution)/shard_map/dot_general | solution.py:81
  93.0 1.8 %fusion.12 = f32[384,512]{1,0:T(8,128)S(1)} fusion(bf16[1024,512]{1,0:T(8,128)(2,1)} %collective-permute-done.4, bf16[384,4096]{1,0:T(8,128)(2,1)S(1)} %copy-done, s32[]{:T(128)S(6)} %select_n.179), kind=kOutput, calls=%fused_computation.36 | convolution fusion | flops 402653184 | bytes 2621444 | tf_op jit(solution)/shard_map/dot_general | solution.py:81
  94.9 0.6 convolution_add_fusion.1
  95.4 1.7 %collective-permute-done.5 = bf16[512,512]{1,0:T(8,128)(2,1)S(1)} collective-permute-done((bf16[512,512]{1,0:T(8,128)(2,1)S(1)}, bf16[512,512]{1,0:T(8,128)(2,1)S(1)}, u32[]{:S(2)}, u32[]{:S(2)}) %collective-permute-start.5) | collective-permute-done | bytes 524320 | tf_op jit(solution)/shard_map/ppermute | solution.py:12
  97.1 6.6 %collective-permute-done.6 = bf16[512,512]{1,0:T(8,128)(2,1)S(1)} collective-permute-done((bf16[512,512]{1,0:T(8,128)(2,1)S(1)}, bf16[512,512]{1,0:T(8,128)(2,1)S(1)}, u32[]{:S(2)}, u32[]{:S(2)}) %collective-permute-start.6) | collective-permute-done | bytes 524320 | tf_op jit(solution)/shard_map/ppermute | solution.py:12
  103.7 1.8 %multiply_convert_fusion = (bf16[384,512]{1,0:T(8,128)(2,1)}, bf16[384,512]{1,0:T(8,128)(2,1)}) fusion(bf16[384,512]{1,0:T(8,128)(2,1)S(1)} %copy-done.11, bf16[384,512]{1,0:T(8,128)(2,1)S(1)} %copy-done.12, f32[384,512]{1,0:T(8,128)S(1)} %fusion.12, f32[384,512]{1,0:T(8,128)S(1)} %convolution_add_fusion.1, ...), kind=kOutput, calls=%fused_computation.35 | convolution fusion | flops 408092672 | bytes 4980740 | tf_op jit(solution)/shard_map/dot_general | solution.py:81
  105.5 1.4 %convert_reduce_fusion = f32[256,512]{0,1:T(8,128)S(1)} fusion(bf16[4,256,512]{1,2,0:T(8,128)(2,1)} %all-to-all-done), kind=kLoop, calls=%fused_computation | loop fusion | flops 917504 | bytes 1572864 | tf_op jit(solution)/shard_map/reduce_sum | solution.py:75
  106.9 0.8 copy.9
  (30 shorter events, 0.1 us)
Async XLA Ops:
  0.6 1.9 %copy-start = (bf16[384,4096]{1,0:T(8,128)(2,1)S(1)}, bf16[384,4096]{1,0:T(8,128)(2,1)}, u32[]{:S(2)}) copy-start(bf16[384,4096]{1,0:T(8,128)(2,1)} %param.4) | copy-start | bytes 9437188
  8.6 1.8 %copy-start.4 = (f32[1024,512]{0,1:T(8,128)}, f32[1024,512]{0,1:T(8,128)S(1)}, u32[]{:S(2)}) copy-start(f32[1024,512]{0,1:T(8,128)S(1)} %get-tuple-element.12) | copy-start | bytes 6291460
  8.6 4.6 %copy-start.2 = (f32[1024,512]{0,1:T(8,128)}, f32[1024,512]{0,1:T(8,128)S(1)}, u32[]{:S(2)}) copy-start(f32[1024,512]{0,1:T(8,128)S(1)} %get-tuple-element.10) | copy-start | bytes 6291460
  10.3 8.4 %copy-start.13 = (bf16[256,512]{1,0:T(8,128)(2,1)S(1)}, bf16[256,512]{1,0:T(8,128)(2,1)}, u32[]{:S(2)}) copy-start(bf16[256,512]{1,0:T(8,128)(2,1)} %param.7) | copy-start | bytes 786436
  10.3 28.4 %collective-permute-start.9 = (bf16[1024,512]{0,1:T(8,128)(2,1)}, bf16[1024,512]{0,1:T(8,128)(2,1)}, u32[]{:S(2)}, u32[]{:S(2)}) collective-permute-start(bf16[1024,512]{0,1:T(8,128)(2,1)} %pad_maximum_fusion.2), channel_id=1, source_target_pairs={{0,384},{128,0},{256,128},{384,256},{1,385},{129,1},{257,129},{385... | collective-permute-start | bytes 3145736 | tf_op jit(solution)/shard_map/ppermute | solution.py:12
  14.5 27.8 %collective-permute-start.7 = (bf16[1024,512]{0,1:T(8,128)(2,1)}, bf16[1024,512]{0,1:T(8,128)(2,1)}, u32[]{:S(2)}, u32[]{:S(2)}) collective-permute-start(bf16[1024,512]{0,1:T(8,128)(2,1)} %pad_maximum_fusion.1), channel_id=1, source_target_pairs={{0,128},{128,256},{256,384},{384,0},{1,129},{129,257},{257,385},{3... | collective-permute-start | bytes 3145736 | tf_op jit(solution)/shard_map/ppermute | solution.py:12
  18.8 30.0 %collective-permute-start = (bf16[256,512]{1,0:T(8,128)(2,1)S(1)}, bf16[256,512]{1,0:T(8,128)(2,1)}, u32[]{:S(2)}, u32[]{:S(2)}) collective-permute-start(bf16[256,512]{1,0:T(8,128)(2,1)S(1)} %copy-done.13), channel_id=1, source_target_pairs={{0,32},{32,64},{64,96},{96,0},{1,33},{33,65},{65,97},{97,1},{2,34}... | collective-permute-start | bytes 786440 | tf_op jit(solution)/shard_map/ppermute | solution.py:12
  22.3 26.5 %collective-permute-start.1 = (bf16[256,512]{1,0:T(8,128)(2,1)S(1)}, bf16[256,512]{1,0:T(8,128)(2,1)}, u32[]{:S(2)}, u32[]{:S(2)}) collective-permute-start(bf16[256,512]{1,0:T(8,128)(2,1)S(1)} %copy-done.13), channel_id=1, source_target_pairs={{0,64},{32,96},{64,0},{96,32},{1,65},{33,97},{65,1},{97,33},{2,66}... | collective-permute-start | bytes 786440 | tf_op jit(solution)/shard_map/ppermute | solution.py:12
  26.8 22.0 %collective-permute-start.2 = (bf16[256,512]{1,0:T(8,128)(2,1)S(1)}, bf16[256,512]{1,0:T(8,128)(2,1)}, u32[]{:S(2)}, u32[]{:S(2)}) collective-permute-start(bf16[256,512]{1,0:T(8,128)(2,1)S(1)} %copy-done.13), channel_id=1, source_target_pairs={{0,96},{32,0},{64,32},{96,64},{1,97},{33,1},{65,33},{97,65},{2,98}... | collective-permute-start | bytes 786440 | tf_op jit(solution)/shard_map/ppermute | solution.py:12
  30.1 12.1 %copy-start.3 = (f32[1024,512]{0,1:T(8,128)S(1)}, f32[1024,512]{0,1:T(8,128)}, u32[]{:S(2)}) copy-start(f32[1024,512]{0,1:T(8,128)} %copy-done.2) | copy-start | bytes 6291460
  30.1 18.6 %copy-start.14 = (bf16[256,512]{1,0:T(8,128)(2,1)S(1)}, bf16[256,512]{1,0:T(8,128)(2,1)}, u32[]{:S(2)}) copy-start(bf16[256,512]{1,0:T(8,128)(2,1)} %param.7) | copy-start | bytes 786436
  40.3 16.7 %collective-permute-start.10 = (bf16[512,512]{0,1:T(8,128)(2,1)S(1)}, bf16[512,512]{0,1:T(8,128)(2,1)S(1)}, u32[]{:S(2)}, u32[]{:S(2)}) collective-permute-start(bf16[512,512]{0,1:T(8,128)(2,1)S(1)} %add_convert_fusion.1), channel_id=1, source_target_pairs={{0,384},{128,0},{256,128},{384,256},{1,385},{129,1},{257,129},{385... | collective-permute-start | bytes 1572872 | tf_op jit(solution)/shard_map/ppermute | solution.py:12
  43.5 17.6 %copy-start.1 = (f32[1024,512]{0,1:T(8,128)S(1)}, f32[1024,512]{0,1:T(8,128)}, u32[]{:S(2)}) copy-start(f32[1024,512]{0,1:T(8,128)} %get-tuple-element.9) | copy-start | bytes 6291460
  43.5 17.6 %collective-permute-start.8 = (bf16[512,512]{0,1:T(8,128)(2,1)S(1)}, bf16[512,512]{0,1:T(8,128)(2,1)S(1)}, u32[]{:S(2)}, u32[]{:S(2)}) collective-permute-start(bf16[512,512]{0,1:T(8,128)(2,1)S(1)} %add_convert_fusion.3), channel_id=1, source_target_pairs={{0,128},{128,256},{256,384},{384,0},{1,129},{129,257},{257,385},{3... | collective-permute-start | bytes 1572872 | tf_op jit(solution)/shard_map/ppermute | solution.py:12
  50.0 7.0 %copy-start.5 = (bf16[256,512]{1,0:T(8,128)(2,1)}, bf16[256,512]{1,0:T(8,128)(2,1)S(1)}, u32[]{:S(2)}) copy-start(bf16[256,512]{1,0:T(8,128)(2,1)S(1)} %get-tuple-element.26) | copy-start | bytes 786436
  50.0 7.0 %copy-start.7 = (bf16[256,512]{1,0:T(8,128)(2,1)}, bf16[256,512]{1,0:T(8,128)(2,1)S(1)}, u32[]{:S(2)}) copy-start(bf16[256,512]{1,0:T(8,128)(2,1)S(1)} %get-tuple-element.27) | copy-start | bytes 786436
  50.0 7.0 %copy-start.9 = (bf16[256,512]{1,0:T(8,128)(2,1)}, bf16[256,512]{1,0:T(8,128)(2,1)S(1)}, u32[]{:S(2)}) copy-start(bf16[256,512]{1,0:T(8,128)(2,1)S(1)} %get-tuple-element.28) | copy-start | bytes 786436
  51.2 30.1 %collective-permute-start.4 = (bf16[1024,512]{1,0:T(8,128)(2,1)}, bf16[1024,512]{1,0:T(8,128)(2,1)}, u32[]{:S(2)}, u32[]{:S(2)}) collective-permute-start(bf16[1024,512]{1,0:T(8,128)(2,1)} %pad_maximum_fusion), channel_id=1, source_target_pairs={{0,128},{128,256},{256,384},{384,0},{1,129},{129,257},{257,385},{3... | collective-permute-start | bytes 3145736 | tf_op jit(solution)/shard_map/ppermute | solution.py:12
  53.1 34.9 %collective-permute-start.3 = (bf16[1024,512]{1,0:T(8,128)(2,1)}, bf16[1024,512]{1,0:T(8,128)(2,1)}, u32[]{:S(2)}, u32[]{:S(2)}) collective-permute-start(bf16[1024,512]{1,0:T(8,128)(2,1)} %pad_maximum_fusion), channel_id=1, source_target_pairs={{0,384},{128,0},{256,128},{384,256},{1,385},{129,1},{257,129},{385... | collective-permute-start | bytes 3145736 | tf_op jit(solution)/shard_map/ppermute | solution.py:12
  63.9 41.6 %all-to-all-start = ((bf16[4,256,512]{1,2,0:T(8,128)(2,1)}), bf16[4,256,512]{1,2,0:T(8,128)(2,1)}, u32[]{:S(2)}, u32[]{:S(2)}) async-start(bf16[4,256,512]{1,2,0:T(8,128)(2,1)} %bitcast.15), calls=%async_computation | async-start | bytes 2097152 | tf_op jit(solution)/shard_map/all_to_all | solution.py:74
  82.4 14.7 %collective-permute-start.5 = (bf16[512,512]{1,0:T(8,128)(2,1)S(1)}, bf16[512,512]{1,0:T(8,128)(2,1)S(1)}, u32[]{:S(2)}, u32[]{:S(2)}) collective-permute-start(bf16[512,512]{1,0:T(8,128)(2,1)S(1)} %slice.60), channel_id=1, source_target_pairs={{0,128},{128,256},{256,384},{384,0},{1,129},{129,257},{257,385},{3... | collective-permute-start | bytes 1572872 | tf_op jit(solution)/shard_map/ppermute | solution.py:12
  89.1 5.7 %copy-start.6 = (bf16[256,512]{1,0:T(8,128)(2,1)S(1)}, bf16[256,512]{1,0:T(8,128)(2,1)}, u32[]{:S(2)}) copy-start(bf16[256,512]{1,0:T(8,128)(2,1)} %copy-done.5) | copy-start | bytes 786436
  89.1 5.7 %copy-start.8 = (bf16[256,512]{1,0:T(8,128)(2,1)S(1)}, bf16[256,512]{1,0:T(8,128)(2,1)}, u32[]{:S(2)}) copy-start(bf16[256,512]{1,0:T(8,128)(2,1)} %copy-done.7) | copy-start | bytes 786436
  89.1 5.7 %copy-start.10 = (bf16[256,512]{1,0:T(8,128)(2,1)S(1)}, bf16[256,512]{1,0:T(8,128)(2,1)}, u32[]{:S(2)}) copy-start(bf16[256,512]{1,0:T(8,128)(2,1)} %copy-done.9) | copy-start | bytes 786436
  89.1 14.5 %collective-permute-start.6 = (bf16[512,512]{1,0:T(8,128)(2,1)S(1)}, bf16[512,512]{1,0:T(8,128)(2,1)S(1)}, u32[]{:S(2)}, u32[]{:S(2)}) collective-permute-start(bf16[512,512]{1,0:T(8,128)(2,1)S(1)} %slice.61), channel_id=1, source_target_pairs={{0,384},{128,0},{256,128},{384,256},{1,385},{129,1},{257,129},{385... | collective-permute-start | bytes 1572872 | tf_op jit(solution)/shard_map/ppermute | solution.py:12
  94.8 8.8 %copy-start.11 = (bf16[384,512]{1,0:T(8,128)(2,1)S(1)}, bf16[384,512]{1,0:T(8,128)(2,1)}, u32[]{:S(2)}) copy-start(bf16[384,512]{1,0:T(8,128)(2,1)} %param.5) | copy-start | bytes 1179652
  94.8 8.8 %copy-start.12 = (bf16[384,512]{1,0:T(8,128)(2,1)S(1)}, bf16[384,512]{1,0:T(8,128)(2,1)}, u32[]{:S(2)}) copy-start(bf16[384,512]{1,0:T(8,128)(2,1)} %param.6) | copy-start | bytes 1179652
